TPU v7x, 512 devices: a whole 4x4x16 slice. The times are simulated.
512 devices in a mesh: seq: 128 (over y, z, core), head: 4 (over x).
Axes of the slice: x: 4, y: 4, z: 16, core: 2. Of those that a mesh axis runs over, the one named last changes fastest.
Arguments:
- tokens: bfloat16 [64, 4, 1024], P('head'), may hold values from -6 to 6
- cache_keys: bfloat16 [64, 4096, 512], P(None, 'seq', 'head'), may hold values from -70 to 70
- cache_values: bfloat16 [64, 4096, 512], P(None, 'seq', 'head'), may hold values from -6 to 6
- held_states: bfloat16 [64, 512, 1024], P(None, 'seq'), may hold values from -6 to 6
- recompute_pos: int32 [64, 512], P(None, 'seq'), may hold values from 0 to 4095, as said below
- cache_len: int32 [64], replicated, may hold values from 1 to 4096
- new_prompt: int32 [64], replicated, may hold values 0 or 1
- w_qkv: bfloat16 [3, 1024, 512], P(None, None, 'head'), may hold values from -0.1875 to 0.1875
- qkv_bias: float32 [3, 512], P(None, 'head'), may hold values from -3 to 3
- w_out: bfloat16 [512, 1024], P('head'), may hold values from -1.5 to 1.5
- out_bias: float32 [1024], replicated, may hold values from -3 to 3
- attn_gain: float32 [1024], replicated, may hold values from 0.1 to 1.9
- attn_shift: float32 [1024], replicated, may hold values from -3 to 3
- w_up: bfloat16 [1024, 2048], P(None, 'head'), may hold values from -0.1875 to 0.1875
- up_bias: float32 [2048], P('head'), may hold values from -3 to 3
- w_down: bfloat16 [2048, 1024], P('head'), may hold values from -0.125 to 0.125
- down_bias: float32 [1024], replicated, may hold values from -3 to 3
- ffn_gain: float32 [1024], replicated, may hold values from 0.1 to 1.9
- ffn_shift: float32 [1024], replicated, may hold values from -3 to 3
Outputs:
- layer_out: bfloat16 [64, 4, 1024], P('head')
Inputs may be any that keep to these rules, and one draw needn't show every extreme that they name: `recompute_pos`: columns s * 4 to (s + 1) * 4 - 1 of a row hold distinct positions from s * 32 to (s + 1) * 32 - 1.
All inputs are finite; a program needn't handle non-finite values.
Results may differ from a plain program's by a relative error of at most 0.011.
Values may be sent and summed in bfloat16 or wider, within the bound.
No kernel may reach another device: no remote copies, remote signals or barrier semaphores. Data moves between devices by JAX's collectives and lax.ppermute only.
A program may use at most 192 MiB of HBM per device.

v0:
```python
import jax
import jax.numpy as jnp
from jax import lax
from jax.sharding import PartitionSpec as P

HDIM = 64


NEG = -1e30
EPS = 1e-05


def layer_norm(values, norm_gain, norm_bias):
    center = jnp.mean(values, axis=-1, keepdims=True)
    spread = values - center
    second = jnp.mean(spread * spread, axis=-1, keepdims=True)
    return spread * lax.rsqrt(second + EPS) * norm_gain + norm_bias


def merge_pair(first_part, second_part):
    first_max, first_sum, first_out = first_part
    second_max, second_sum, second_out = second_part
    joint_max = jnp.maximum(first_max, second_max)
    first_scale = jnp.exp(first_max - joint_max)
    second_scale = jnp.exp(second_max - joint_max)
    return (
        joint_max,
        first_sum * first_scale + second_sum * second_scale,
        first_out * first_scale[..., None] + second_out * second_scale[..., None],
    )


def partial_attention(queries, keys_here, values_here, visible):
    scores = jnp.einsum(
        "rthe,rphe->rthp", queries, keys_here, preferred_element_type=jnp.float32
    ) * HDIM ** (-0.5)
    highest = jnp.max(jnp.where(visible, scores, NEG), axis=-1)
    weights = jnp.exp(jnp.where(visible, scores - highest[..., None], NEG)).astype(jnp.bfloat16)
    totals = jnp.sum(weights.astype(jnp.float32), axis=-1)
    blended = jnp.einsum(
        "rthp,rphe->rthe", weights, values_here, preferred_element_type=jnp.float32
    )
    return (highest, totals, blended)


def on_device(
    tokens,
    cache_keys,
    cache_values,
    held_states,
    recompute_pos,
    cache_len,
    new_prompt,
    w_qkv,
    qkv_bias,
    w_out,
    out_bias,
    attn_gain,
    attn_shift,
    w_up,
    up_bias,
    w_down,
    down_bias,
    ffn_gain,
    ffn_shift,
):
    local_width = w_qkv.shape[2]
    local_heads = local_width // HDIM
    requests = cache_keys.shape[0]
    block_len = cache_keys.shape[1]
    own_rows = tokens.shape[0]
    steps_count = tokens.shape[1]
    block_rows = lax.all_gather(tokens, "head", axis=0, tiled=True)
    triple = (
        jnp.einsum("rtd,kdc->rtkc", block_rows, w_qkv, preferred_element_type=jnp.float32)
        + qkv_bias
    )
    triple = triple.astype(jnp.bfloat16).reshape(
        block_rows.shape[0], block_rows.shape[1], 3 * local_width
    )
    gathered = jnp.concatenate([triple, block_rows], axis=2)
    head_shape = (requests, steps_count, local_heads, HDIM)
    queries = gathered[:, :, :local_width].reshape(head_shape)
    new_keys = gathered[:, :, local_width : 2 * local_width].reshape(head_shape)
    new_values = gathered[:, :, 2 * local_width : 3 * local_width].reshape(head_shape)
    fresh_keys = (
        jnp.einsum("rjd,dc->rjc", held_states, w_qkv[1], preferred_element_type=jnp.float32)
        + qkv_bias[1]
    ).astype(jnp.bfloat16)
    offset_pos = lax.axis_index("seq") * block_len
    positions = jnp.arange(block_len, dtype=jnp.int32)
    matches = (recompute_pos - offset_pos)[:, :, None] == positions[None, None, :]
    placed = jnp.einsum(
        "rjp,rjc->rpc", matches.astype(jnp.bfloat16), fresh_keys, preferred_element_type=jnp.float32
    ).astype(jnp.bfloat16)
    replaced = jnp.any(matches, axis=1)
    keys_here = jnp.where(replaced[:, :, None], placed, cache_keys).reshape(
        requests, block_len, local_heads, HDIM
    )
    values_here = cache_values.reshape(requests, block_len, local_heads, HDIM)
    visible = ((offset_pos + positions)[None, :] < cache_len[:, None]) & (new_prompt[:, None] == 0)
    block_max, block_sum, block_out = partial_attention(
        queries, keys_here, values_here, visible[:, None, None, :]
    )
    cache_max = lax.pmax(block_max, "seq")
    factor = jnp.exp(block_max - cache_max)
    cache_sum, cache_out = lax.psum((block_sum * factor, block_out * factor[..., None]), "seq")
    order_t = jnp.arange(steps_count, dtype=jnp.int32)
    causal = (order_t[:, None] >= order_t[None, :])[None, :, None, :]
    new_max, new_sum, new_out = partial_attention(queries, new_keys, new_values, causal)
    joint_max, joint_sum, joint_out = merge_pair(
        (cache_max, cache_sum, cache_out), (new_max, new_sum, new_out)
    )
    attended = (
        (joint_out / joint_sum[..., None])
        .astype(jnp.bfloat16)
        .reshape(requests, steps_count, local_width)
    )
    head_terms = jnp.einsum("rtc,cd->rtd", attended, w_out, preferred_element_type=jnp.float32)
    summed = lax.psum(head_terms, "head")
    inputs_all = gathered[:, :, 3 * local_width :]
    normed_all = layer_norm(
        inputs_all.astype(jnp.float32) + summed + out_bias, attn_gain, attn_shift
    ).astype(jnp.bfloat16)
    hidden_all = jax.nn.gelu(
        jnp.einsum("rtd,df->rtf", normed_all, w_up, preferred_element_type=jnp.float32) + up_bias,
        approximate=False,
    ).astype(jnp.bfloat16)
    normed = lax.dynamic_slice_in_dim(normed_all, lax.axis_index("head") * own_rows, own_rows, 0)
    reduced = lax.psum_scatter(
        jnp.einsum("rtf,fd->rtd", hidden_all, w_down, preferred_element_type=jnp.float32),
        "head",
        scatter_dimension=0,
        tiled=True,
    )
    return layer_norm(normed.astype(jnp.float32) + reduced + down_bias, ffn_gain, ffn_shift).astype(
        jnp.bfloat16
    )


def solution(mesh):
    placed = (
        P("head", None, None),
        P(None, "seq", "head"),
        P(None, "seq", "head"),
        P(None, "seq", None),
        P(None, "seq"),
        P(),
        P(),
        P(None, None, "head"),
        P(None, "head"),
        P("head", None),
        P(),
        P(),
        P(),
        P(None, "head"),
        P("head"),
        P("head", None),
        P(),
        P(),
        P(),
    )
    return jax.shard_map(
        on_device, mesh=mesh, in_specs=placed, out_specs=P("head", None, None), check_vma=False
    )
```

profile of v0, /device:TPU:1, one launch (start us, length us, event | category | flops | bytes accessed | tf_op | source)
XLA Modules:
  0.0 721.5 jit_solution(1206370637751851345)
XLA Ops:
  6.5 0.8 copy-done.17
  7.3 0.1 copy.60
  7.4 0.2 fusion.67
  7.6 0.5 copy-done.16
  8.1 1.5 fusion.9
  9.6 0.9 fusion
  10.5 0.0 copy-start.9
  10.5 0.4 reshape.114
  11.0 0.5 copy-done.9
  11.5 11.2 %all_gather.3 = bf16[64,4,1024]{2,0,1:T(8,128)(2,1)S(1)} all-gather(bf16[16,4,1024]{2,0,1:T(8,128)(2,1)S(1)} %copy.59), channel_id=1, replica_groups=mesh['seq'=128,'head'=4] {'head'}, dimensions={0}, use_global_device_ids=true | all-gather | bytes 655360 | tf_op jit(solution)/shard_map/all_gather | solution.py:73
  22.7 0.4 fusion.8
  23.2 0.7 fusion.119
  23.8 0.1 reshape.116
  23.9 0.5 copy-done.22
  24.5 0.6 copy-done.18
  25.1 0.1 compare_and_fusion
  25.2 0.8 select_reduce_fusion
  26.1 0.1 copy.68
  26.2 0.4 convert_reduce_fusion
  26.6 0.1 copy.79
  26.7 256.7 %pmax.7 = f32[64,4,2]{0,1,2:T(4,128)S(1)} all-reduce(f32[64,4,2]{0,1,2:T(4,128)S(1)} %copy.68), channel_id=1, replica_groups=mesh['seq'=128,'head'=4] {'seq'}, use_global_device_ids=true, to_apply=%region_2.3 | all-reduce | flops 512 | bytes 4096 | tf_op jit(solution)/shard_map/pmax | solution.py:105
  283.4 0.7 copy.69
  284.1 0.4 reshape.117
  284.6 2.0 fusion.5
  286.6 0.0 all-reduce.3.cloned.1.call-update
  286.6 0.0 copy-start.8
  286.6 0.0 all-reduce.5.cloned.1.call-start
  286.7 249.5 %psum.22 = f32[64,4,2]{0,1,2:T(4,128)S(1)} all-reduce(f32[64,4,2]{0,1,2:T(4,128)S(1)} %bitcast.79), channel_id=1, replica_groups=mesh['seq'=128,'head'=4] {'seq'}, use_global_device_ids=true, to_apply=%region_6.7 | all-reduce | flops 512 | bytes 4096 | tf_op jit(solution)/shard_map/psum | solution.py:107
  536.2 0.1 reshape.118
  536.3 0.3 fusion.65
  536.6 0.1 copy.72
  536.8 0.1 fusion.77
  536.9 0.1 convert_reduce_fusion.1
  537.0 0.1 copy.74
  537.1 0.1 copy.78
  537.2 0.1 copy.81
  537.4 0.2 copy.76
  537.5 0.1 reshape.119
  537.7 73.2 %all-reduce.3.cloned.1.call-done = f32[64,4,2,64]{3,1,2,0:T(4,128)} async-done(((f32[64,4,2,64]{3,1,2,0:T(4,128)}), f32[64,4,2,64]{3,1,2,0:T(4,128)}) %all-reduce.3.cloned.1.call-update) | async-done | bytes 131088 | tf_op jit(solution)/shard_map/psum | solution.py:107
  610.9 1.4 fusion.7
  612.3 0.0 copy-start.6
  612.4 0.1 copy.82
  612.5 0.1 reshape.120
  612.6 0.7 copy-done.6
  613.3 1.3 fusion.30
  614.6 0.0 all-reduce.5.cloned.1.call-update
  614.6 0.0 reduce-scatter.2.cloned.1.call-start
  614.7 57.6 %all-reduce.5.cloned.1.call-done = f32[64,4,1024]{2,0,1:T(8,128)} async-done(((f32[64,4,1024]{2,0,1:T(8,128)}), f32[64,4,1024]{2,0,1:T(8,128)}) %all-reduce.5.cloned.1.call-update) | async-done | bytes 1048592 | tf_op jit(solution)/shard_map/psum | solution.py:120
  672.3 1.5 fusion.27
  673.8 0.0 copy-start.13
  673.8 0.3 multiply_reduce_fusion
  674.2 0.4 copy-done.13
  674.5 0.3 copy-done.12
  674.8 0.3 add_convert_fusion
  675.1 0.9 copy-done.19
  676.1 0.6 fusion.69
  676.6 2.5 fusion.10
  679.1 0.0 reduce-scatter.2.cloned.1.call-update
  679.2 32.9 %reduce-scatter.2.cloned.1.call-done = f32[16,4,1024]{2,0,1:T(8,128)} async-done(((f32[64,4,1024]{2,0,1:T(8,128)}), f32[16,4,1024]{2,0,1:T(8,128)}) %reduce-scatter.2.cloned.1.call-update) | async-done | bytes 262160 | tf_op jit(solution)/shard_map/reduce_scatter | solution.py:130
  712.1 1.1 fusion.76
  713.3 0.2 multiply_reduce_fusion.1
  713.5 0.7 copy-done.14
  714.1 0.1 add_convert_fusion.1
  714.2 0.8 copy.83
  (46 shorter events, 0.2 us)
Async XLA Ops:
  6.5 670.1 %copy-start = (bf16[512,1024]{1,0:T(8,128)(2,1)S(1)}, bf16[512,1024]{1,0:T(8,128)(2,1)}, u32[]{:S(2)}) copy-start(bf16[512,1024]{1,0:T(8,128)(2,1)} %param.34) | copy-start | bytes 3145732
  6.5 604.4 %all-reduce.3.cloned.1.call-start = ((), (), s32[]{:S(2)}) async-start(), calls=%async_computation.1 | async-start | bytes 524288 | tf_op jit(solution)/shard_map/psum | solution.py:107
  6.5 0.8 copy-start.17
  7.4 0.7 copy-start.16
  8.1 1.5 copy-start.20
  10.5 0.9 copy-start.9
  11.4 11.2 %copy-start.3 = (bf16[3,1024,128]{2,1,0:T(8,128)(2,1)S(1)}, bf16[3,1024,128]{2,1,0:T(8,128)(2,1)}, u32[]{:S(2)}) copy-start(bf16[3,1024,128]{2,1,0:T(8,128)(2,1)} %param.26) | copy-start | bytes 2359300
  23.8 0.7 copy-start.22
  24.5 0.7 copy-start.7
  24.5 0.7 copy-start.18
  26.1 258.1 %copy-start.4 = (bf16[64,32,128]{2,1,0:T(8,128)(2,1)S(1)}, bf16[64,32,128]{2,1,0:T(8,128)(2,1)}, u32[]{:S(2)}) copy-start(bf16[64,32,128]{2,1,0:T(8,128)(2,1)} %param.21) | copy-start | bytes 1572868
  286.6 249.7 %copy-start.5 = (bf16[64,4,128]{2,0,1:T(8,128)(2,1)S(1)}, bf16[64,4,128]{2,0,1:T(8,128)(2,1)}, u32[]{:S(2)}) copy-start(bf16[64,4,128]{2,0,1:T(8,128)(2,1)} %get-tuple-element.15) | copy-start | bytes 196612
  286.6 249.7 %copy-start.8 = (bf16[64,4,2,64]{3,2,0,1:T(2,128)(2,1)S(1)}, bf16[64,4,2,64]{3,2,0,1:T(2,128)(2,1)}, u32[]{:S(2)}) copy-start(bf16[64,4,2,64]{3,2,0,1:T(2,128)(2,1)} %copy-done.7) | copy-start | bytes 196612
  286.6 385.7 %all-reduce.5.cloned.1.call-start = ((), (), s32[]{:S(2)}) async-start(), calls=%async_computation.2 | async-start | bytes 2097152 | tf_op jit(solution)/shard_map/psum | solution.py:120
  612.3 1.0 copy-start.6
  614.6 57.7 %copy-start.10 = (f32[1024]{0:T(1024)S(1)}, f32[1024]{0:T(1024)}, u32[]{:S(2)}) copy-start(f32[1024]{0:T(1024)} %param.29) | copy-start | bytes 12292
  614.6 97.5 %reduce-scatter.2.cloned.1.call-start = ((), (), s32[]{:S(2)}) async-start(), calls=%async_computation.3 | async-start | bytes 1310720 | tf_op jit(solution)/shard_map/reduce_scatter | solution.py:130
  672.3 1.5 copy-start.1
  673.8 0.7 copy-start.13
  674.1 0.7 copy-start.12
  674.8 1.2 copy-start.19
  674.8 1.2 copy-start.21
  679.2 32.9 %copy-start.11 = (f32[1024]{0:T(1024)S(1)}, f32[1024]{0:T(1024)}, u32[]{:S(2)}) copy-start(f32[1024]{0:T(1024)} %param.35) | copy-start | bytes 12292
  712.1 1.1 copy-start.2
  712.1 1.4 copy-start.15
  713.4 0.7 copy-start.14
Sparse Core Ops, SparseCore 0:
  286.7 324.1 all-reduce.2
  614.8 57.4 all-reduce.4
  679.3 32.7 reduce-scatter.1
where the time goes:
time: 723 us; the launch traced here: 722 us
  blocking collectives  517 us (72%)
  waiting for transfers between devices  164 us (23%)
  between operations  13.4 us (2%)
  matrix products  11.8 us (2%)
  local copies, waits for them, and re-layouts  10.5 us (1%)
    pmax x1, blocking collectives, on_device(): cache_max = lax.pmax(block_max, 'seq')  257 us
    psum x1, blocking collectives, on_device(): lax.psum((block_sum * factor, block_out * factor[..., None]), 'seq')  250 us
    psum x1, waiting for transfers between devices, on_device(): lax.psum((block_sum * factor, block_out * factor[..., None]), 'seq')  73.2 us
    psum x1, waiting for transfers between devices, on_device(): summed = lax.psum(head_terms, 'head')  57.6 us
    reduce_scatter x1, waiting for transfers between devices, on_device(): lax.psum_scatter(jnp.einsum('rtf,fd->rtd', hidden_all, w_down, preferred_...  32.9 us
  transfers between devices with their start and end apart: 3, of which 3 were waited for; matrix products, arithmetic and copies ran while one was open for 0% of the time, Pallas kernels for 0%

commit v1 on v0

--- a/solution.py
+++ b/solution.py
@@ -41,6 +41,40 @@
         "rthp,rphe->rthe", weights, values_here, preferred_element_type=jnp.float32
     )
     return (highest, totals, blended)
+
+
+def seq_merge(block_max, block_sum, block_out):
+    n_seq = lax.axis_size("seq")
+    head_shape = block_out.shape
+    lanes = head_shape[-2] * head_shape[-1]
+    rows = block_out.size // lanes
+    stat_rows = block_max.size // lanes
+    out2 = block_out.reshape(rows, lanes)
+    top = block_max.reshape(stat_rows, lanes)
+    total = block_sum.reshape(stat_rows, lanes)
+    width = head_shape[-1]
+    step = 1
+    while step < n_seq:
+        pairs = [(i, i ^ step) for i in range(n_seq)]
+        packed = jnp.concatenate([out2, top, total], axis=0)
+        other = lax.ppermute(packed, "seq", pairs)
+        o_out = other[:rows]
+        o_top = other[rows : rows + stat_rows]
+        o_total = other[rows + stat_rows :]
+        joint = jnp.maximum(top, o_top)
+        mine = jnp.exp(top - joint)
+        theirs = jnp.exp(o_top - joint)
+        total = total * mine + o_total * theirs
+        mine_rows = jnp.repeat(mine.reshape(rows, lanes // width), width, axis=1)
+        theirs_rows = jnp.repeat(theirs.reshape(rows, lanes // width), width, axis=1)
+        out2 = out2 * mine_rows + o_out * theirs_rows
+        top = joint
+        step *= 2
+    return (
+        top.reshape(block_max.shape),
+        total.reshape(block_sum.shape),
+        out2.reshape(head_shape),
+    )
 
 
 def on_device(
@@ -102,9 +136,7 @@
     block_max, block_sum, block_out = partial_attention(
         queries, keys_here, values_here, visible[:, None, None, :]
     )
-    cache_max = lax.pmax(block_max, "seq")
-    factor = jnp.exp(block_max - cache_max)
-    cache_sum, cache_out = lax.psum((block_sum * factor, block_out * factor[..., None]), "seq")
+    cache_max, cache_sum, cache_out = seq_merge(block_max, block_sum, block_out)
     order_t = jnp.arange(steps_count, dtype=jnp.int32)
     causal = (order_t[:, None] >= order_t[None, :])[None, :, None, :]
     new_max, new_sum, new_out = partial_attention(queries, new_keys, new_values, causal)

time: 723 us -> 233 us (0.32)
  blocking collectives: 517 us -> 11.1 us
  starting transfers between devices: 0.09 us -> 33.7 us
  waiting for transfers between devices: 164 us -> 141 us
    pmax x1 -> x0, blocking collectives: 257 us -> none  [on_device(): cache_max = lax.pmax(block_max, 'seq')]
    psum x1 -> x0, blocking collectives: 250 us -> none  [on_device(): lax.psum((block_sum * factor, block_out * factor[..., None]), 'seq')]
    psum x1 -> x0, waiting for transfers between devices: 73.2 us -> none  [on_device(): lax.psum((block_sum * factor, block_out * factor[..., None]), 'seq')]
    ppermute x0 -> x7, waiting for transfers between devices: none -> 51 us  [seq_merge(): other = lax.ppermute(packed, 'seq', pairs)]
    ppermute x0 -> x7, starting transfers between devices: none -> 33.4 us  [seq_merge(): other = lax.ppermute(packed, 'seq', pairs)]
  transfers between devices with their start and end apart: 3 -> 9, of which waited for: 3 -> 9; matrix products, arithmetic and copies ran while one was open for 0% -> 0% of each run, Pallas kernels for 0% -> 0%
where the time goes in v1:
time: 233 us; the launch traced here: 232 us
  waiting for transfers between devices  141 us (61%)
  starting transfers between devices  33.7 us (14%)
  local copies, waits for them, and re-layouts  16.8 us (7%)
  between operations  14.3 us (6%)
  blocking collectives  11.1 us (5%)
  matrix products  8.92 us (4%)
  other arithmetic  6.39 us (3%)
    psum x1, waiting for transfers between devices, on_device(): summed = lax.psum(head_terms, 'head')  56.9 us
    ppermute x7, waiting for transfers between devices, seq_merge(): other = lax.ppermute(packed, 'seq', pairs)  51 us
    ppermute x7, starting transfers between devices, seq_merge(): other = lax.ppermute(packed, 'seq', pairs)  33.4 us
    reduce_scatter x1, waiting for transfers between devices, on_device(): lax.psum_scatter(jnp.einsum('rtf,fd->rtd', hidden_all, w_down, preferred_...  32.9 us
    all_gather x1, blocking collectives, on_device(): block_rows = lax.all_gather(tokens, 'head', axis=0, tiled=True)  11.1 us
    unnamed x41, local copies, waits for them, and re-layouts  4.99 us
  transfers between devices with their start and end apart: 9, of which 9 were waited for; matrix products, arithmetic and copies ran while one was open for 0% of the time, Pallas kernels for 0%

profile of v1, /device:TPU:1, one launch (start us, length us, event | category | flops | bytes accessed | tf_op | source)
XLA Modules:
  0.0 232.0 jit_solution(7463980318247415298)
XLA Ops:
  6.5 0.8 broadcast_compare_fusion
  7.3 0.7 slice_bitcast_fusion
  8.0 0.7 broadcast_subtract_fusion
  8.8 0.2 fusion.73
  9.0 1.0 copy.122
  10.0 11.1 %all_gather.3 = bf16[64,4,1024]{2,0,1:T(8,128)(2,1)S(1)} all-gather(bf16[16,4,1024]{2,0,1:T(8,128)(2,1)S(1)} %copy.122), channel_id=1, replica_groups=mesh['seq'=128,'head'=4] {'head'}, dimensions={0}, use_global_device_ids=true | all-gather | bytes 655360 | tf_op jit(solution)/shard_map/all_gather | solution.py:107
  21.0 0.4 fusion.7
  21.5 0.7 fusion.131
  22.2 0.8 reshape.249
  23.0 0.3 fusion.8
  23.3 0.7 copy-done.18
  24.0 0.9 fusion
  24.9 0.4 reshape.247
  25.3 0.2 copy-done.15
  25.7 1.7 select_reduce_fusion
  27.4 0.5 copy.131
  27.9 0.4 convert_reduce_fusion
  28.3 0.5 copy.132
  28.8 0.2 reshape.253
  29.0 0.2 reshape.252
  29.1 0.4 reshape.250
  29.5 0.4 convolution_bitcast_fusion.1
  30.1 0.2 reshape.251
  30.3 10.5 %collective-permute-start = (f32[264,128]{1,0:T(8,128)S(1)}, f32[264,128]{1,0:T(8,128)S(1)}, u32[]{:S(2)}, u32[]{:S(2)}) collective-permute-start(f32[264,128]{1,0:T(8,128)S(1)} %pad_maximum_fusion), channel_id=1, source_target_pairs={{0,4},{4,0},{8,12},{12,8},{16,20},{20,16},{24,28},{28,24},{32,36},... | collective-permute-start | bytes 405512 | tf_op jit(solution)/shard_map/ppermute | solution.py:60
  40.8 1.0 collective-permute-done
  42.1 0.1 reshape.256
  42.5 1.9 collective-permute-start.1
  44.5 4.7 %collective-permute-done.1 = f32[264,128]{1,0:T(8,128)S(1)} collective-permute-done((f32[264,128]{1,0:T(8,128)S(1)}, f32[264,128]{1,0:T(8,128)S(1)}, u32[]{:S(2)}, u32[]{:S(2)}) %collective-permute-start.1) | collective-permute-done | bytes 135200 | tf_op jit(solution)/shard_map/ppermute | solution.py:60
  49.6 0.1 reshape.260
  50.0 1.9 collective-permute-start.2
  51.9 9.3 %collective-permute-done.2 = f32[264,128]{1,0:T(8,128)S(1)} collective-permute-done((f32[264,128]{1,0:T(8,128)S(1)}, f32[264,128]{1,0:T(8,128)S(1)}, u32[]{:S(2)}, u32[]{:S(2)}) %collective-permute-start.2) | collective-permute-done | bytes 135200 | tf_op jit(solution)/shard_map/ppermute | solution.py:60
  61.5 0.1 reshape.264
  61.9 3.8 %collective-permute-start.3 = (f32[264,128]{1,0:T(8,128)S(1)}, f32[264,128]{1,0:T(8,128)S(1)}, u32[]{:S(2)}, u32[]{:S(2)}) collective-permute-start(f32[264,128]{1,0:T(8,128)S(1)} %pad_maximum_fusion.3), channel_id=1, source_target_pairs={{0,32},{4,36},{8,40},{12,44},{16,48},{20,52},{24,56},{28,60},{32,0... | collective-permute-start | bytes 405512 | tf_op jit(solution)/shard_map/ppermute | solution.py:60
  65.9 13.8 %collective-permute-done.3 = f32[264,128]{1,0:T(8,128)S(1)} collective-permute-done((f32[264,128]{1,0:T(8,128)S(1)}, f32[264,128]{1,0:T(8,128)S(1)}, u32[]{:S(2)}, u32[]{:S(2)}) %collective-permute-start.3) | collective-permute-done | bytes 135200 | tf_op jit(solution)/shard_map/ppermute | solution.py:60
  80.4 11.0 %collective-permute-start.4 = (f32[264,128]{1,0:T(8,128)S(1)}, f32[264,128]{1,0:T(8,128)S(1)}, u32[]{:S(2)}, u32[]{:S(2)}) collective-permute-start(f32[264,128]{1,0:T(8,128)S(1)} %pad_maximum_fusion.4), channel_id=1, source_target_pairs={{0,64},{4,68},{8,72},{12,76},{16,80},{20,84},{24,88},{28,92},{32,9... | collective-permute-start | bytes 405512 | tf_op jit(solution)/shard_map/ppermute | solution.py:60
  91.4 0.3 fusion.71
  91.7 13.5 %collective-permute-done.4 = f32[264,128]{1,0:T(8,128)S(1)} collective-permute-done((f32[264,128]{1,0:T(8,128)S(1)}, f32[264,128]{1,0:T(8,128)S(1)}, u32[]{:S(2)}, u32[]{:S(2)}) %collective-permute-start.4) | collective-permute-done | bytes 135200 | tf_op jit(solution)/shard_map/ppermute | solution.py:60
  106.0 1.9 collective-permute-start.5
  108.3 4.2 %collective-permute-done.5 = f32[264,128]{1,0:T(8,128)S(1)} collective-permute-done((f32[264,128]{1,0:T(8,128)S(1)}, f32[264,128]{1,0:T(8,128)S(1)}, u32[]{:S(2)}, u32[]{:S(2)}) %collective-permute-start.5) | collective-permute-done | bytes 135200 | tf_op jit(solution)/shard_map/ppermute | solution.py:60
  113.3 2.4 %collective-permute-start.6 = (f32[264,128]{1,0:T(8,128)S(1)}, f32[264,128]{1,0:T(8,128)S(1)}, u32[]{:S(2)}, u32[]{:S(2)}) collective-permute-start(f32[264,128]{1,0:T(8,128)S(1)} %pad_maximum_fusion.6), channel_id=1, source_target_pairs={{0,256},{4,260},{8,264},{12,268},{16,272},{20,276},{24,280},{28,28... | collective-permute-start | bytes 405512 | tf_op jit(solution)/shard_map/ppermute | solution.py:60
  115.8 0.2 copy.172
  116.0 4.6 %collective-permute-done.6 = f32[264,128]{1,0:T(8,128)S(1)} collective-permute-done((f32[264,128]{1,0:T(8,128)S(1)}, f32[264,128]{1,0:T(8,128)S(1)}, u32[]{:S(2)}, u32[]{:S(2)}) %collective-permute-start.6) | collective-permute-done | bytes 135200 | tf_op jit(solution)/shard_map/ppermute | solution.py:60
  120.5 0.2 reshape.286
  120.8 0.2 reshape.278
  121.6 0.2 reshape.282
  121.8 0.2 reshape.283
  122.5 0.5 fusion.6
  123.2 0.7 copy-done.6
  124.0 1.3 fusion.29
  125.3 0.2 reduce-scatter.2.cloned.1.call-start
  125.5 56.9 %all-reduce.2.cloned.1.call-done = f32[64,4,1024]{2,0,1:T(8,128)} async-done(((f32[64,4,1024]{2,0,1:T(8,128)}), f32[64,4,1024]{2,0,1:T(8,128)}) %all-reduce.2.cloned.1.call-update) | async-done | bytes 1048592 | tf_op jit(solution)/shard_map/psum | solution.py:152
  182.5 1.5 fusion.26
  184.0 0.3 multiply_reduce_fusion
  184.3 0.4 copy-done.11
  184.7 0.3 copy-done.10
  185.0 0.3 add_convert_fusion
  185.3 0.9 copy-done.16
  186.2 0.6 fusion.75
  186.8 2.5 %fusion.9 = f32[64,4,1024]{2,0,1:T(8,128)} fusion(bf16[512,1024]{1,0:T(8,128)(2,1)S(1)} %copy-done, f32[64,4,512]{2,0,1:T(8,128)S(1)} %get-tuple-element.45, u8[64,512]{1,0:T(8,128)(4,1)S(1)} %get-tuple-element.6, u8[64,512]{1,0:T(8,128)(4,1)S(1)} %get-tuple-element.5), kind=kOutput, calls=%fused_computation.16 | convolution fusion | flops 277610496 | bytes 2686976 | tf_op jit(solution)/shard_map/rtf,fd->rtd/dot_general | solution.py:163
  189.4 32.9 %reduce-scatter.2.cloned.1.call-done = f32[16,4,1024]{2,0,1:T(8,128)} async-done(((f32[64,4,1024]{2,0,1:T(8,128)}), f32[16,4,1024]{2,0,1:T(8,128)}) %reduce-scatter.2.cloned.1.call-update) | async-done | bytes 262160 | tf_op jit(solution)/shard_map/reduce_scatter | solution.py:162
  222.3 1.1 fusion.82
  223.4 0.2 multiply_reduce_fusion.1
  223.6 0.7 copy-done.12
  224.4 0.8 copy.180
  (133 shorter events, 6.3 us)
Async XLA Ops:
  6.5 180.3 %copy-start = (bf16[512,1024]{1,0:T(8,128)(2,1)S(1)}, bf16[512,1024]{1,0:T(8,128)(2,1)}, u32[]{:S(2)}) copy-start(bf16[512,1024]{1,0:T(8,128)(2,1)} %param.34) | copy-start | bytes 3145732
  6.5 14.5 %copy-start.3 = (bf16[3,1024,128]{2,1,0:T(8,128)(2,1)S(1)}, bf16[3,1024,128]{2,1,0:T(8,128)(2,1)}, u32[]{:S(2)}) copy-start(bf16[3,1024,128]{2,1,0:T(8,128)(2,1)} %param.26) | copy-start | bytes 2359300
  6.5 175.9 %all-reduce.2.cloned.1.call-start = ((), (), s32[]{:S(2)}) async-start(), calls=%async_computation.1 | async-start | bytes 2097152 | tf_op jit(solution)/shard_map/psum | solution.py:152
  9.9 11.1 %copy-start.14 = (f32[3,128]{1,0:T(4,128)S(1)}, f32[3,128]{1,0:T(4,128)}, u32[]{:S(2)}) copy-start(f32[3,128]{1,0:T(4,128)} %param.27) | copy-start | bytes 4612
  21.5 1.5 copy-start.17
  23.0 1.0 copy-start.18
  24.9 0.7 copy-start.15
  27.4 1.8 copy-start.4
  30.3 11.4 %collective-permute-start = (f32[264,128]{1,0:T(8,128)S(1)}, f32[264,128]{1,0:T(8,128)S(1)}, u32[]{:S(2)}, u32[]{:S(2)}) collective-permute-start(f32[264,128]{1,0:T(8,128)S(1)} %pad_maximum_fusion), channel_id=1, source_target_pairs={{0,4},{4,0},{8,12},{12,8},{16,20},{20,16},{24,28},{28,24},{32,36},... | collective-permute-start | bytes 405512 | tf_op jit(solution)/shard_map/ppermute | solution.py:60
  42.5 6.7 %collective-permute-start.1 = (f32[264,128]{1,0:T(8,128)S(1)}, f32[264,128]{1,0:T(8,128)S(1)}, u32[]{:S(2)}, u32[]{:S(2)}) collective-permute-start(f32[264,128]{1,0:T(8,128)S(1)} %pad_maximum_fusion.1), channel_id=1, source_target_pairs={{0,8},{4,12},{8,0},{12,4},{16,24},{20,28},{24,16},{28,20},{32,40},... | collective-permute-start | bytes 405512 | tf_op jit(solution)/shard_map/ppermute | solution.py:60
  50.0 11.2 %collective-permute-start.2 = (f32[264,128]{1,0:T(8,128)S(1)}, f32[264,128]{1,0:T(8,128)S(1)}, u32[]{:S(2)}, u32[]{:S(2)}) collective-permute-start(f32[264,128]{1,0:T(8,128)S(1)} %pad_maximum_fusion.2), channel_id=1, source_target_pairs={{0,16},{4,20},{8,24},{12,28},{16,0},{20,4},{24,8},{28,12},{32,48},... | collective-permute-start | bytes 405512 | tf_op jit(solution)/shard_map/ppermute | solution.py:60
  61.9 3.9 %copy-start.5 = (bf16[64,4,128]{2,0,1:T(8,128)(2,1)S(1)}, bf16[64,4,128]{2,0,1:T(8,128)(2,1)}, u32[]{:S(2)}) copy-start(bf16[64,4,128]{2,0,1:T(8,128)(2,1)} %get-tuple-element.41) | copy-start | bytes 196612
  61.9 17.7 %collective-permute-start.3 = (f32[264,128]{1,0:T(8,128)S(1)}, f32[264,128]{1,0:T(8,128)S(1)}, u32[]{:S(2)}, u32[]{:S(2)}) collective-permute-start(f32[264,128]{1,0:T(8,128)S(1)} %pad_maximum_fusion.3), channel_id=1, source_target_pairs={{0,32},{4,36},{8,40},{12,44},{16,48},{20,52},{24,56},{28,60},{32,0... | collective-permute-start | bytes 405512 | tf_op jit(solution)/shard_map/ppermute | solution.py:60
  80.4 11.0 %copy-start.7 = (bf16[64,4,2,64]{3,2,0,1:T(2,128)(2,1)S(1)}, bf16[64,4,2,64]{3,2,0,1:T(2,128)(2,1)}, u32[]{:S(2)}) copy-start(bf16[64,4,2,64]{3,2,0,1:T(2,128)(2,1)} %reshape.249) | copy-start | bytes 196612
  80.4 24.8 %collective-permute-start.4 = (f32[264,128]{1,0:T(8,128)S(1)}, f32[264,128]{1,0:T(8,128)S(1)}, u32[]{:S(2)}, u32[]{:S(2)}) collective-permute-start(f32[264,128]{1,0:T(8,128)S(1)} %pad_maximum_fusion.4), channel_id=1, source_target_pairs={{0,64},{4,68},{8,72},{12,76},{16,80},{20,84},{24,88},{28,92},{32,9... | collective-permute-start | bytes 405512 | tf_op jit(solution)/shard_map/ppermute | solution.py:60
  106.0 6.5 %collective-permute-start.5 = (f32[264,128]{1,0:T(8,128)S(1)}, f32[264,128]{1,0:T(8,128)S(1)}, u32[]{:S(2)}, u32[]{:S(2)}) collective-permute-start(f32[264,128]{1,0:T(8,128)S(1)} %pad_maximum_fusion.5), channel_id=1, source_target_pairs={{0,128},{4,132},{8,136},{12,140},{16,144},{20,148},{24,152},{28,15... | collective-permute-start | bytes 405512 | tf_op jit(solution)/shard_map/ppermute | solution.py:60
  113.3 7.3 %collective-permute-start.6 = (f32[264,128]{1,0:T(8,128)S(1)}, f32[264,128]{1,0:T(8,128)S(1)}, u32[]{:S(2)}, u32[]{:S(2)}) collective-permute-start(f32[264,128]{1,0:T(8,128)S(1)} %pad_maximum_fusion.6), channel_id=1, source_target_pairs={{0,256},{4,260},{8,264},{12,268},{16,272},{20,276},{24,280},{28,28... | collective-permute-start | bytes 405512 | tf_op jit(solution)/shard_map/ppermute | solution.py:60
  123.0 1.0 copy-start.6
  125.3 57.2 %copy-start.8 = (f32[1024]{0:T(1024)S(1)}, f32[1024]{0:T(1024)}, u32[]{:S(2)}) copy-start(f32[1024]{0:T(1024)} %param.29) | copy-start | bytes 12292
  125.3 97.0 %reduce-scatter.2.cloned.1.call-start = ((), (), s32[]{:S(2)}) async-start(), calls=%async_computation.2 | async-start | bytes 1310720 | tf_op jit(solution)/shard_map/reduce_scatter | solution.py:162
  182.5 1.5 copy-start.1
  184.0 0.7 copy-start.11
  184.3 0.7 copy-start.10
  185.0 1.2 copy-start.16
  185.0 1.2 copy-start.19
  189.3 32.9 %copy-start.9 = (f32[1024]{0:T(1024)S(1)}, f32[1024]{0:T(1024)}, u32[]{:S(2)}) copy-start(f32[1024]{0:T(1024)} %param.35) | copy-start | bytes 12292
  222.3 1.1 copy-start.2
  222.3 1.4 copy-start.13
  223.6 0.7 copy-start.12
Sparse Core Ops, SparseCore 0:
  125.4 56.9 all-reduce.1
  189.5 32.7 reduce-scatter.1

commit v2 on v1

--- a/solution.py
+++ b/solution.py
@@ -148,27 +148,26 @@
         .astype(jnp.bfloat16)
         .reshape(requests, steps_count, local_width)
     )
-    head_terms = jnp.einsum("rtc,cd->rtd", attended, w_out, preferred_element_type=jnp.float32)
-    summed = lax.psum(head_terms, "head")
-    inputs_all = gathered[:, :, 3 * local_width :]
-    normed_all = layer_norm(
-        inputs_all.astype(jnp.float32) + summed + out_bias, attn_gain, attn_shift
+    w_out_all = lax.all_gather(w_out, "head", axis=0, tiled=True)
+    w_up_all = lax.all_gather(w_up, "head", axis=0)
+    up_bias_all = lax.all_gather(up_bias, "head", axis=0)
+    w_down_all = lax.all_gather(w_down, "head", axis=0)
+    own_attended = lax.all_to_all(attended, "head", 0, 2, tiled=True)
+    projected = jnp.einsum(
+        "rtc,cd->rtd", own_attended, w_out_all, preferred_element_type=jnp.float32
+    )
+    normed = layer_norm(
+        tokens.astype(jnp.float32) + projected + out_bias, attn_gain, attn_shift
     ).astype(jnp.bfloat16)
-    hidden_all = jax.nn.gelu(
-        jnp.einsum("rtd,df->rtf", normed_all, w_up, preferred_element_type=jnp.float32) + up_bias,
+    hidden = jax.nn.gelu(
+        jnp.einsum("rtd,hdf->rthf", normed, w_up_all, preferred_element_type=jnp.float32)
+        + up_bias_all,
         approximate=False,
     ).astype(jnp.bfloat16)
-    normed = lax.dynamic_slice_in_dim(normed_all, lax.axis_index("head") * own_rows, own_rows, 0)
-    reduced = lax.psum_scatter(
-        jnp.einsum("rtf,fd->rtd", hidden_all, w_down, preferred_element_type=jnp.float32),
-        "head",
-        scatter_dimension=0,
-        tiled=True,
-    )
-    return layer_norm(normed.astype(jnp.float32) + reduced + down_bias, ffn_gain, ffn_shift).astype(
+    lowered = jnp.einsum("rthf,hfd->rtd", hidden, w_down_all, preferred_element_type=jnp.float32)
+    return layer_norm(normed.astype(jnp.float32) + lowered + down_bias, ffn_gain, ffn_shift).astype(
         jnp.bfloat16
     )
-
 
 def solution(mesh):
     placed = (

time: 233 us -> 177 us (0.76)
  waiting for transfers between devices: 141 us -> 75.4 us
  blocking collectives: 11.1 us -> 21.3 us
  matrix products: 8.92 us -> 14.7 us
  local copies, waits for them, and re-layouts: 16.8 us -> 11.3 us
  other arithmetic: 6.39 us -> 2.48 us
  starting transfers between devices: 33.7 us -> 36.7 us
    psum x1 -> x0, waiting for transfers between devices: 56.9 us -> none  [on_device(): summed = lax.psum(head_terms, 'head')]
    reduce_scatter x1 -> x0, waiting for transfers between devices: 32.9 us -> none  [on_device(): lax.psum_scatter(jnp.einsum('rtf,fd->rtd', hidden_all, w_down, preferred_...]
    all_gather x0 -> x3, waiting for transfers between devices: none -> 23 us  [the longest x1 23 us: on_device(): w_down_all = lax.all_gather(w_down, 'head', axis=0)]
    all_gather x0 -> x1, blocking collectives: none -> 10.2 us  [on_device(): up_bias_all = lax.all_gather(up_bias, 'head', axis=0)]
    unnamed x41 -> x28, local copies, waits for them, and re-layouts: 4.99 us -> 0.11 us
    dot_general x3, matrix products: 4.37 us -> 8.94 us  [the longest x1 4.12 us: on_device(): jnp.einsum('rthf,hfd->rtd', hidden, w_down_all, preferred_element_type=jn...]
    all_to_all x0 -> x1, starting transfers between devices: none -> 3.29 us  [on_device(): own_attended = lax.all_to_all(attended, 'head', 0, 2, tiled=True)]
    reduce_sum x2 -> x0, other arithmetic: 2.67 us -> none  [layer_norm(): center = jnp.mean(values, axis=-1, keepdims=True)]
  transfers between devices with their start and end apart: 9 -> 11, of which waited for: 9 -> 8; matrix products, arithmetic and copies ran while one was open for 0% -> 13% of each run, Pallas kernels for 0% -> 0%
where the time goes in v2:
time: 177 us; the launch traced here: 176 us
  waiting for transfers between devices  75.4 us (43%)
  starting transfers between devices  36.7 us (21%)
  blocking collectives  21.3 us (12%)
  matrix products  14.7 us (8%)
  between operations  14 us (8%)
  local copies, waits for them, and re-layouts  11.3 us (6%)
  other arithmetic  2.48 us (1%)
    ppermute x7, waiting for transfers between devices, seq_merge(): other = lax.ppermute(packed, 'seq', pairs)  50.9 us
    ppermute x7, starting transfers between devices, seq_merge(): other = lax.ppermute(packed, 'seq', pairs)  33.3 us
    all_gather x1, waiting for transfers between devices, on_device(): w_down_all = lax.all_gather(w_down, 'head', axis=0)  23 us
    all_gather x1, blocking collectives, on_device(): block_rows = lax.all_gather(tokens, 'head', axis=0, tiled=True)  11.1 us
    all_gather x1, blocking collectives, on_device(): up_bias_all = lax.all_gather(up_bias, 'head', axis=0)  10.2 us
    dot_general x1, matrix products, on_device(): jnp.einsum('rthf,hfd->rtd', hidden, w_down_all, preferred_element_type=jn...  4.12 us
  transfers between devices with their start and end apart: 11, of which 8 were waited for; matrix products, arithmetic and copies ran while one was open for 13% of the time, Pallas kernels for 0%

profile of v2, /device:TPU:1, one launch (start us, length us, event | category | flops | bytes accessed | tf_op | source)
XLA Modules:
  0.0 176.0 jit_solution(12113696045356791960)
XLA Ops:
  6.5 0.7 all-gather.8.cloned.1.call-update
  7.3 0.7 all-gather.10.cloned.1.call-update
  8.1 0.7 broadcast_subtract_fusion
  8.9 0.2 fusion.72
  9.0 0.7 slice_bitcast_fusion
  9.7 1.4 fusion.11
  11.2 1.9 %fusion = bf16[64,32,128]{2,1,0:T(8,128)(2,1)S(1)} fusion(bf16[64,32,128]{2,1,0:T(8,128)(2,1)} %param.20, pred[64,32]{1,0:T(8,128)(4,1)S(1)} %fusion.72, bf16[64,4,128]{2,0,1:T(8,128)(2,1)S(1)} %fusion.11, s32[64,4]{1,0:T(8,128)S(1)} %copy.130), kind=kOutput, calls=%fused_computation.1 | convolution fusion | flops 2629632 | bytes 1117184 | tf_op jit(solution)/shard_map/rjp,rjc->rpc/dot_general | solution.py:127
  13.1 0.4 reshape.247
  13.5 11.1 %all_gather.24 = bf16[64,4,1024]{2,0,1:T(8,128)(2,1)S(1)} all-gather(bf16[16,4,1024]{2,0,1:T(8,128)(2,1)S(1)} %copy.129), channel_id=1, replica_groups=mesh['seq'=128,'head'=4] {'head'}, dimensions={0}, use_global_device_ids=true | all-gather | bytes 655360 | tf_op jit(solution)/shard_map/all_gather | solution.py:107
  24.6 0.4 fusion.10
  25.3 0.4 reshape.250
  25.8 0.8 select_reduce_fusion
  26.6 0.5 copy.139
  27.1 0.5 convolution_bitcast_fusion.2
  27.7 0.2 reshape.251
  27.9 0.4 convert_reduce_fusion
  28.3 0.5 copy.140
  28.8 0.2 reshape.253
  29.0 0.2 reshape.252
  29.2 10.5 %collective-permute-start = (f32[264,128]{1,0:T(8,128)S(1)}, f32[264,128]{1,0:T(8,128)S(1)}, u32[]{:S(2)}, u32[]{:S(2)}) collective-permute-start(f32[264,128]{1,0:T(8,128)S(1)} %pad_maximum_fusion), channel_id=1, source_target_pairs={{0,4},{4,0},{8,12},{12,8},{16,20},{20,16},{24,28},{28,24},{32,36},... | collective-permute-start | bytes 405512 | tf_op jit(solution)/shard_map/ppermute | solution.py:60
  39.6 1.0 collective-permute-done
  40.6 0.1 reshape.254
  41.0 0.1 reshape.256
  41.4 1.9 %collective-permute-start.1 = (f32[264,128]{1,0:T(8,128)S(1)}, f32[264,128]{1,0:T(8,128)S(1)}, u32[]{:S(2)}, u32[]{:S(2)}) collective-permute-start(f32[264,128]{1,0:T(8,128)S(1)} %pad_maximum_fusion.1), channel_id=1, source_target_pairs={{0,8},{4,12},{8,0},{12,4},{16,24},{20,28},{24,16},{28,20},{32,40},... | collective-permute-start | bytes 405512 | tf_op jit(solution)/shard_map/ppermute | solution.py:60
  43.3 4.7 %collective-permute-done.1 = f32[264,128]{1,0:T(8,128)S(1)} collective-permute-done((f32[264,128]{1,0:T(8,128)S(1)}, f32[264,128]{1,0:T(8,128)S(1)}, u32[]{:S(2)}, u32[]{:S(2)}) %collective-permute-start.1) | collective-permute-done | bytes 135200 | tf_op jit(solution)/shard_map/ppermute | solution.py:60
  48.1 0.1 reshape.258
  48.4 0.1 reshape.260
  48.8 1.9 %collective-permute-start.2 = (f32[264,128]{1,0:T(8,128)S(1)}, f32[264,128]{1,0:T(8,128)S(1)}, u32[]{:S(2)}, u32[]{:S(2)}) collective-permute-start(f32[264,128]{1,0:T(8,128)S(1)} %pad_maximum_fusion.2), channel_id=1, source_target_pairs={{0,16},{4,20},{8,24},{12,28},{16,0},{20,4},{24,8},{28,12},{32,48},... | collective-permute-start | bytes 405512 | tf_op jit(solution)/shard_map/ppermute | solution.py:60
  50.7 9.3 %collective-permute-done.2 = f32[264,128]{1,0:T(8,128)S(1)} collective-permute-done((f32[264,128]{1,0:T(8,128)S(1)}, f32[264,128]{1,0:T(8,128)S(1)}, u32[]{:S(2)}, u32[]{:S(2)}) %collective-permute-start.2) | collective-permute-done | bytes 135200 | tf_op jit(solution)/shard_map/ppermute | solution.py:60
  60.0 0.1 reshape.262
  60.4 0.1 reshape.264
  60.8 3.9 %collective-permute-start.3 = (f32[264,128]{1,0:T(8,128)S(1)}, f32[264,128]{1,0:T(8,128)S(1)}, u32[]{:S(2)}, u32[]{:S(2)}) collective-permute-start(f32[264,128]{1,0:T(8,128)S(1)} %pad_maximum_fusion.3), channel_id=1, source_target_pairs={{0,32},{4,36},{8,40},{12,44},{16,48},{20,52},{24,56},{28,60},{32,0... | collective-permute-start | bytes 405512 | tf_op jit(solution)/shard_map/ppermute | solution.py:60
  64.8 13.8 %collective-permute-done.3 = f32[264,128]{1,0:T(8,128)S(1)} collective-permute-done((f32[264,128]{1,0:T(8,128)S(1)}, f32[264,128]{1,0:T(8,128)S(1)}, u32[]{:S(2)}, u32[]{:S(2)}) %collective-permute-start.3) | collective-permute-done | bytes 135200 | tf_op jit(solution)/shard_map/ppermute | solution.py:60
  78.6 0.1 reshape.266
  78.9 0.1 reshape.268
  79.4 10.7 %collective-permute-start.4 = (f32[264,128]{1,0:T(8,128)S(1)}, f32[264,128]{1,0:T(8,128)S(1)}, u32[]{:S(2)}, u32[]{:S(2)}) collective-permute-start(f32[264,128]{1,0:T(8,128)S(1)} %pad_maximum_fusion.4), channel_id=1, source_target_pairs={{0,64},{4,68},{8,72},{12,76},{16,80},{20,84},{24,88},{28,92},{32,9... | collective-permute-start | bytes 405512 | tf_op jit(solution)/shard_map/ppermute | solution.py:60
  90.1 0.3 fusion.70
  90.4 13.5 %collective-permute-done.4 = f32[264,128]{1,0:T(8,128)S(1)} collective-permute-done((f32[264,128]{1,0:T(8,128)S(1)}, f32[264,128]{1,0:T(8,128)S(1)}, u32[]{:S(2)}, u32[]{:S(2)}) %collective-permute-start.4) | collective-permute-done | bytes 135200 | tf_op jit(solution)/shard_map/ppermute | solution.py:60
  103.9 0.1 reshape.270
  104.3 0.1 reshape.272
  104.7 1.9 %collective-permute-start.5 = (f32[264,128]{1,0:T(8,128)S(1)}, f32[264,128]{1,0:T(8,128)S(1)}, u32[]{:S(2)}, u32[]{:S(2)}) collective-permute-start(f32[264,128]{1,0:T(8,128)S(1)} %pad_maximum_fusion.5), channel_id=1, source_target_pairs={{0,128},{4,132},{8,136},{12,140},{16,144},{20,148},{24,152},{28,15... | collective-permute-start | bytes 405512 | tf_op jit(solution)/shard_map/ppermute | solution.py:60
  106.6 0.1 copy.171
  106.9 4.3 %collective-permute-done.5 = f32[264,128]{1,0:T(8,128)S(1)} collective-permute-done((f32[264,128]{1,0:T(8,128)S(1)}, f32[264,128]{1,0:T(8,128)S(1)}, u32[]{:S(2)}, u32[]{:S(2)}) %collective-permute-start.5) | collective-permute-done | bytes 135200 | tf_op jit(solution)/shard_map/ppermute | solution.py:60
  111.1 0.1 reshape.274
  111.5 0.1 reshape.276
  111.9 2.4 %collective-permute-start.6 = (f32[264,128]{1,0:T(8,128)S(1)}, f32[264,128]{1,0:T(8,128)S(1)}, u32[]{:S(2)}, u32[]{:S(2)}) collective-permute-start(f32[264,128]{1,0:T(8,128)S(1)} %pad_maximum_fusion.6), channel_id=1, source_target_pairs={{0,256},{4,260},{8,264},{12,268},{16,272},{20,276},{24,280},{28,28... | collective-permute-start | bytes 405512 | tf_op jit(solution)/shard_map/ppermute | solution.py:60
  114.4 0.2 copy.180
  114.7 4.4 %collective-permute-done.6 = f32[264,128]{1,0:T(8,128)S(1)} collective-permute-done((f32[264,128]{1,0:T(8,128)S(1)}, f32[264,128]{1,0:T(8,128)S(1)}, u32[]{:S(2)}, u32[]{:S(2)}) %collective-permute-start.6) | collective-permute-done | bytes 135200 | tf_op jit(solution)/shard_map/ppermute | solution.py:60
  119.2 0.2 reshape.283
  119.5 0.2 reshape.286
  120.2 0.1 reshape.278
  120.5 0.1 reshape.280
  120.9 0.2 reshape.282
  121.2 0.5 fusion.9
  121.8 0.7 reshape.302
  122.5 3.3 %all-to-all-start = ((bf16[64,4,128]{2,1,0:T(4,128)(2,1)}), bf16[64,4,128]{2,1,0:T(4,128)(2,1)S(1)}, u32[]{:S(2)}, u32[]{:S(2)}) async-start(bf16[64,4,128]{2,1,0:T(4,128)(2,1)} %reshape.302), calls=%async_computation | async-start | bytes 131072 | tf_op jit(solution)/shard_map/all_to_all | solution.py:155
  125.8 10.2 %all-gather.3 = f32[4,1,512]{2,1,0:T(1,128)S(1)} all-gather(f32[1,1,512]{2,1,0:T(1,128)S(1)} %bitcast.123), channel_id=3, replica_groups=mesh['seq'=128,'head'=4] {'head'}, dimensions={0}, use_global_device_ids=true | all-gather | bytes 10240 | tf_op jit(solution)/shard_map/all_gather | solution.py:153
  136.1 1.6 fusion.132
  137.8 0.2 multiply_reduce_fusion.1
  138.0 3.2 %fusion.74 = (u8[16,4,512]{2,0,1:T(8,128)(4,1)S(1)}, u8[16,4,512]{2,0,1:T(8,128)(4,1)S(1)}, f32[16,4,4,512]{3,0,2,1:T(8,128)S(1)}) fusion(f32[4,512]{1,0:T(4,128)S(1)} %bitcast.122, bf16[4,1024,512,1]{2,1,0,3:T(8,128)(2,1)} %bitcast.124, f32[1024]{0:T(1024)S(1)} %copy-done.10, f32[1024]{0:T(1024)S(1)} %copy-done.11, f32[16,4]{0,1:T(4,128)S(1)} %add_rsqrt_fusion.1, ...), kind=kOutput, calls=%fused_computation.119 | convolution fusion | flops 270532608 | bytes 5063168 | tf_op jit(solution)/shard_map/rtd,hdf->rthf/dot_general | solution.py:163
  141.2 23.0 %all-gather.12.cloned.1.call-done = bf16[2048,1024]{1,0:T(8,128)(2,1)} async-done(((bf16[512,1024]{1,0:T(8,128)(2,1)}), bf16[2048,1024]{1,0:T(8,128)(2,1)}) %all-gather.12.cloned.1.call-update) | async-done | bytes 4194320 | tf_op jit(solution)/shard_map/all_gather | solution.py:154
  164.2 4.1 %fusion.133 = (f32[16,4]{0,1:T(4,128)S(1)}, f32[16,4,1024]{2,0,1:T(8,128)S(1)}) fusion(f32[1024]{0:T(1024)S(1)} %copy-done.9, bf16[4,512,1024,1]{2,1,0,3:T(8,128)(2,1)} %bitcast.125, f32[16,4,4,512]{3,0,2,1:T(8,128)S(1)} %get-tuple-element.47, u8[16,4,512]{2,0,1:T(8,128)(4,1)S(1)} %get-tuple-element.6, u8[16,4,512]{2,0,1:T(8,128)(4,1)S(1)} %get-tuple-element.5, ...), kind=kOutput, calls=%fused_computation.220 | convolution fusion | flops 278200256 | bytes 5321472 | tf_op jit(solution)/shard_map/rthf,hfd->rtd/dot_general | solution.py:167
  168.3 0.2 multiply_reduce_fusion
  168.7 0.8 copy.191
  (124 shorter events, 4.9 us)
Async XLA Ops:
  6.5 18.1 %copy-start.6 = (f32[3,128]{1,0:T(4,128)S(1)}, f32[3,128]{1,0:T(4,128)}, u32[]{:S(2)}) copy-start(f32[3,128]{1,0:T(4,128)} %param.27) | copy-start | bytes 4612
  6.5 18.1 %copy-start = (bf16[3,1024,128]{2,1,0:T(8,128)(2,1)S(1)}, bf16[3,1024,128]{2,1,0:T(8,128)(2,1)}, u32[]{:S(2)}) copy-start(bf16[3,1024,128]{2,1,0:T(8,128)(2,1)} %param.26) | copy-start | bytes 2359300
  6.5 6.9 %copy-start.2 = (bf16[16,4,1024]{2,1,0:T(4,128)(2,1)S(1)}, bf16[16,4,1024]{2,1,0:T(4,128)(2,1)}, u32[]{:S(2)}) copy-start(bf16[16,4,1024]{2,1,0:T(4,128)(2,1)} %param.19) | copy-start | bytes 393220
  6.5 129.6 %all-gather.8.cloned.1.call-start = ((), (), s32[]{:S(2)}) async-start(), calls=%async_computation.1 | async-start | bytes 1310720 | tf_op jit(solution)/shard_map/all_gather | solution.py:151
  7.3 18.0 %copy-start.1 = (bf16[64,32,128]{2,1,0:T(8,128)(2,1)S(1)}, bf16[64,32,128]{2,1,0:T(8,128)(2,1)}, u32[]{:S(2)}) copy-start(bf16[64,32,128]{2,1,0:T(8,128)(2,1)} %param.21) | copy-start | bytes 1572868
  7.3 130.7 %all-gather.10.cloned.1.call-start = ((), (), s32[]{:S(2)}) async-start(), calls=%async_computation.2 | async-start | bytes 5242880 | tf_op jit(solution)/shard_map/all_gather | solution.py:152
  8.0 156.2 %all-gather.12.cloned.1.call-start = ((), (), s32[]{:S(2)}) async-start(), calls=%async_computation.3 | async-start | bytes 5242880 | tf_op jit(solution)/shard_map/all_gather | solution.py:154
  11.1 14.5 %copy-start.12 = (s32[64]{0:T(128)S(1)}, s32[64]{0:T(128)}, u32[]{:S(2)}) copy-start(s32[64]{0:T(128)} %param.25) | copy-start | bytes 772
  11.2 14.5 %copy-start.8 = (s32[64]{0:T(128)S(1)}, s32[64]{0:T(128)}, u32[]{:S(2)}) copy-start(s32[64]{0:T(128)} %param.24) | copy-start | bytes 772
  29.2 11.4 %collective-permute-start = (f32[264,128]{1,0:T(8,128)S(1)}, f32[264,128]{1,0:T(8,128)S(1)}, u32[]{:S(2)}, u32[]{:S(2)}) collective-permute-start(f32[264,128]{1,0:T(8,128)S(1)} %pad_maximum_fusion), channel_id=1, source_target_pairs={{0,4},{4,0},{8,12},{12,8},{16,20},{20,16},{24,28},{28,24},{32,36},... | collective-permute-start | bytes 405512 | tf_op jit(solution)/shard_map/ppermute | solution.py:60
  41.4 6.7 %collective-permute-start.1 = (f32[264,128]{1,0:T(8,128)S(1)}, f32[264,128]{1,0:T(8,128)S(1)}, u32[]{:S(2)}, u32[]{:S(2)}) collective-permute-start(f32[264,128]{1,0:T(8,128)S(1)} %pad_maximum_fusion.1), channel_id=1, source_target_pairs={{0,8},{4,12},{8,0},{12,4},{16,24},{20,28},{24,16},{28,20},{32,40},... | collective-permute-start | bytes 405512 | tf_op jit(solution)/shard_map/ppermute | solution.py:60
  48.8 11.2 %collective-permute-start.2 = (f32[264,128]{1,0:T(8,128)S(1)}, f32[264,128]{1,0:T(8,128)S(1)}, u32[]{:S(2)}, u32[]{:S(2)}) collective-permute-start(f32[264,128]{1,0:T(8,128)S(1)} %pad_maximum_fusion.2), channel_id=1, source_target_pairs={{0,16},{4,20},{8,24},{12,28},{16,0},{20,4},{24,8},{28,12},{32,48},... | collective-permute-start | bytes 405512 | tf_op jit(solution)/shard_map/ppermute | solution.py:60
  60.8 17.8 %collective-permute-start.3 = (f32[264,128]{1,0:T(8,128)S(1)}, f32[264,128]{1,0:T(8,128)S(1)}, u32[]{:S(2)}, u32[]{:S(2)}) collective-permute-start(f32[264,128]{1,0:T(8,128)S(1)} %pad_maximum_fusion.3), channel_id=1, source_target_pairs={{0,32},{4,36},{8,40},{12,44},{16,48},{20,52},{24,56},{28,60},{32,0... | collective-permute-start | bytes 405512 | tf_op jit(solution)/shard_map/ppermute | solution.py:60
  79.4 24.5 %collective-permute-start.4 = (f32[264,128]{1,0:T(8,128)S(1)}, f32[264,128]{1,0:T(8,128)S(1)}, u32[]{:S(2)}, u32[]{:S(2)}) collective-permute-start(f32[264,128]{1,0:T(8,128)S(1)} %pad_maximum_fusion.4), channel_id=1, source_target_pairs={{0,64},{4,68},{8,72},{12,76},{16,80},{20,84},{24,88},{28,92},{32,9... | collective-permute-start | bytes 405512 | tf_op jit(solution)/shard_map/ppermute | solution.py:60
  104.7 6.5 %collective-permute-start.5 = (f32[264,128]{1,0:T(8,128)S(1)}, f32[264,128]{1,0:T(8,128)S(1)}, u32[]{:S(2)}, u32[]{:S(2)}) collective-permute-start(f32[264,128]{1,0:T(8,128)S(1)} %pad_maximum_fusion.5), channel_id=1, source_target_pairs={{0,128},{4,132},{8,136},{12,140},{16,144},{20,148},{24,152},{28,15... | collective-permute-start | bytes 405512 | tf_op jit(solution)/shard_map/ppermute | solution.py:60
  111.9 7.3 %collective-permute-start.6 = (f32[264,128]{1,0:T(8,128)S(1)}, f32[264,128]{1,0:T(8,128)S(1)}, u32[]{:S(2)}, u32[]{:S(2)}) collective-permute-start(f32[264,128]{1,0:T(8,128)S(1)} %pad_maximum_fusion.6), channel_id=1, source_target_pairs={{0,256},{4,260},{8,264},{12,268},{16,272},{20,276},{24,280},{28,28... | collective-permute-start | bytes 405512 | tf_op jit(solution)/shard_map/ppermute | solution.py:60
  121.1 4.7 %copy-start.7 = (f32[512]{0:T(512)S(1)}, f32[512]{0:T(512)}, u32[]{:S(2)}) copy-start(f32[512]{0:T(512)} %param.33) | copy-start | bytes 6148
  121.1 15.0 %copy-start.3 = (f32[1024]{0:T(1024)S(1)}, f32[1024]{0:T(1024)}, u32[]{:S(2)}) copy-start(f32[1024]{0:T(1024)} %param.29) | copy-start | bytes 12292
  121.1 16.9 %copy-start.10 = (f32[1024]{0:T(1024)S(1)}, f32[1024]{0:T(1024)}, u32[]{:S(2)}) copy-start(f32[1024]{0:T(1024)} %param.31) | copy-start | bytes 12292
  121.2 16.9 %copy-start.11 = (f32[1024]{0:T(1024)S(1)}, f32[1024]{0:T(1024)}, u32[]{:S(2)}) copy-start(f32[1024]{0:T(1024)} %param.30) | copy-start | bytes 12292
  122.5 13.5 %all-to-all-start = ((bf16[64,4,128]{2,1,0:T(4,128)(2,1)}), bf16[64,4,128]{2,1,0:T(4,128)(2,1)S(1)}, u32[]{:S(2)}, u32[]{:S(2)}) async-start(bf16[64,4,128]{2,1,0:T(4,128)(2,1)} %reshape.302), calls=%async_computation | async-start | bytes 131072 | tf_op jit(solution)/shard_map/all_to_all | solution.py:155
  137.8 26.4 %copy-start.9 = (f32[1024]{0:T(1024)S(1)}, f32[1024]{0:T(1024)}, u32[]{:S(2)}) copy-start(f32[1024]{0:T(1024)} %param.35) | copy-start | bytes 12292
  164.2 4.3 %copy-start.4 = (f32[1024]{0:T(1024)S(1)}, f32[1024]{0:T(1024)}, u32[]{:S(2)}) copy-start(f32[1024]{0:T(1024)} %param.37) | copy-start | bytes 12292
  164.2 4.3 %copy-start.5 = (f32[1024]{0:T(1024)S(1)}, f32[1024]{0:T(1024)}, u32[]{:S(2)}) copy-start(f32[1024]{0:T(1024)} %param.36) | copy-start | bytes 12292
Sparse Core Ops, SparseCore 0:
  9.4 34.9 all-gather.7
  46.5 58.2 all-gather.9
  106.9 57.2 all-gather.11

commit v3 on v0

--- a/solution.py
+++ b/solution.py
@@ -42,6 +42,81 @@
     )
     return (highest, totals, blended)
 
+
+def merge_rows(mine, theirs, width):
+    top, total, out = mine
+    o_top, o_total, o_out = theirs
+    joint = jnp.maximum(top, o_top)
+    scale = jnp.exp(top - joint)
+    o_scale = jnp.exp(o_top - joint)
+    out = out * jnp.repeat(scale, width, axis=1) + o_out * jnp.repeat(o_scale, width, axis=1)
+    return (joint, total * scale + o_total * o_scale, out)
+
+
+def exchange(stats, pairs):
+    top, total, out = stats
+    rows, heads = top.shape
+    lanes = out.shape[1]
+    flat = jnp.concatenate([top, total], axis=1).reshape(-1)
+    fill = (-flat.size) % lanes
+    flat = jnp.pad(flat, (0, fill)).reshape(-1, lanes)
+    other = lax.ppermute(jnp.concatenate([out, flat], axis=0), "seq", pairs)
+    o_out = other[:rows]
+    o_flat = other[rows:].reshape(-1)[: rows * 2 * heads].reshape(rows, 2 * heads)
+    return (o_flat[:, :heads], o_flat[:, heads:], o_out)
+
+
+def pick(flag, when_set, when_clear):
+    return jax.tree.map(lambda a, b: jnp.where(flag, a, b), when_set, when_clear)
+
+
+def seq_attend(stats, width):
+    n_seq = lax.axis_size("seq")
+    me = lax.axis_index("seq")
+    rows = stats[2].shape[0]
+    bit = 1
+    other = exchange(stats, [(i, i ^ bit) for i in range(n_seq)])
+    stats = merge_rows(stats, other, width)
+    bit *= 2
+    scatter_bits = []
+    while bit < n_seq and rows % 16 == 0 and len(scatter_bits) < 4:
+        half = rows // 2
+        upper = (me // bit) % 2 == 1
+        low = jax.tree.map(lambda a: a[:half], stats)
+        high = jax.tree.map(lambda a: a[half:], stats)
+        keep = pick(upper, high, low)
+        send = pick(upper, low, high)
+        other = exchange(send, [(i, i ^ bit) for i in range(n_seq)])
+        stats = merge_rows(keep, other, width)
+        scatter_bits.append(bit)
+        rows = half
+        bit *= 2
+    while bit < n_seq:
+        other = exchange(stats, [(i, i ^ bit) for i in range(n_seq)])
+        stats = merge_rows(stats, other, width)
+        bit *= 2
+    top, total, out = stats
+    attended = (out / jnp.repeat(total, width, axis=1)).astype(jnp.bfloat16)
+    for bit in reversed(scatter_bits):
+        upper = (me // bit) % 2 == 1
+        other = lax.ppermute(attended, "seq", [(i, i ^ bit) for i in range(n_seq)])
+        attended = jnp.where(
+            upper,
+            jnp.concatenate([other, attended], axis=0),
+            jnp.concatenate([attended, other], axis=0),
+        )
+    return attended
+
+
+def head_gather(x):
+    n_head = lax.axis_size("head")
+    me = lax.axis_index("head")
+    parts = [x]
+    for shift in range(1, n_head):
+        parts.append(lax.ppermute(x, "head", [(i, (i + shift) % n_head) for i in range(n_head)]))
+    stacked = jnp.stack(parts)
+    order = (me - jnp.arange(n_head)) % n_head
+    return jnp.take(stacked, order, axis=0)
 
 def on_device(
     tokens,
@@ -70,7 +145,7 @@
     block_len = cache_keys.shape[1]
     own_rows = tokens.shape[0]
     steps_count = tokens.shape[1]
-    block_rows = lax.all_gather(tokens, "head", axis=0, tiled=True)
+    block_rows = head_gather(tokens).reshape((-1,) + tokens.shape[1:])
     triple = (
         jnp.einsum("rtd,kdc->rtkc", block_rows, w_qkv, preferred_element_type=jnp.float32)
         + qkv_bias
@@ -102,41 +177,36 @@
     block_max, block_sum, block_out = partial_attention(
         queries, keys_here, values_here, visible[:, None, None, :]
     )
-    cache_max = lax.pmax(block_max, "seq")
-    factor = jnp.exp(block_max - cache_max)
-    cache_sum, cache_out = lax.psum((block_sum * factor, block_out * factor[..., None]), "seq")
     order_t = jnp.arange(steps_count, dtype=jnp.int32)
     causal = (order_t[:, None] >= order_t[None, :])[None, :, None, :]
     new_max, new_sum, new_out = partial_attention(queries, new_keys, new_values, causal)
-    joint_max, joint_sum, joint_out = merge_pair(
-        (cache_max, cache_sum, cache_out), (new_max, new_sum, new_out)
-    )
-    attended = (
-        (joint_out / joint_sum[..., None])
-        .astype(jnp.bfloat16)
-        .reshape(requests, steps_count, local_width)
-    )
-    head_terms = jnp.einsum("rtc,cd->rtd", attended, w_out, preferred_element_type=jnp.float32)
-    summed = lax.psum(head_terms, "head")
-    inputs_all = gathered[:, :, 3 * local_width :]
-    normed_all = layer_norm(
-        inputs_all.astype(jnp.float32) + summed + out_bias, attn_gain, attn_shift
-    ).astype(jnp.bfloat16)
-    hidden_all = jax.nn.gelu(
-        jnp.einsum("rtd,df->rtf", normed_all, w_up, preferred_element_type=jnp.float32) + up_bias,
+    rows = requests * steps_count
+    flat = lambda m, s, o: (m.reshape(rows, local_heads), s.reshape(rows, local_heads), o.reshape(rows, local_width))
+    cache_part = flat(block_max, block_sum, block_out)
+    new_part = flat(new_max, new_sum, new_out)
+    first = lax.axis_index("seq") == 0
+    stats = pick(first, merge_rows(cache_part, new_part, HDIM), cache_part)
+    attended = seq_attend(stats, HDIM).reshape(requests, steps_count, local_width)
+    w_out_all = lax.all_gather(w_out, "head", axis=0, tiled=True)
+    w_up_all = lax.all_gather(w_up, "head", axis=0)
+    up_bias_all = head_gather(up_bias)
+    w_down_all = lax.all_gather(w_down, "head", axis=0)
+    own_attended = lax.all_to_all(attended, "head", 0, 2, tiled=True)
+    projected = jnp.einsum(
+        "rtc,cd->rtd", own_attended, w_out_all, preferred_element_type=jnp.float32
+    )
+    normed = layer_norm(
+        tokens.astype(jnp.float32) + projected + out_bias, attn_gain, attn_shift
+    ).astype(jnp.bfloat16)
+    hidden = jax.nn.gelu(
+        jnp.einsum("rtd,hdf->rthf", normed, w_up_all, preferred_element_type=jnp.float32)
+        + up_bias_all,
         approximate=False,
     ).astype(jnp.bfloat16)
-    normed = lax.dynamic_slice_in_dim(normed_all, lax.axis_index("head") * own_rows, own_rows, 0)
-    reduced = lax.psum_scatter(
-        jnp.einsum("rtf,fd->rtd", hidden_all, w_down, preferred_element_type=jnp.float32),
-        "head",
-        scatter_dimension=0,
-        tiled=True,
-    )
-    return layer_norm(normed.astype(jnp.float32) + reduced + down_bias, ffn_gain, ffn_shift).astype(
+    lowered = jnp.einsum("rthf,hfd->rtd", hidden, w_down_all, preferred_element_type=jnp.float32)
+    return layer_norm(normed.astype(jnp.float32) + lowered + down_bias, ffn_gain, ffn_shift).astype(
         jnp.bfloat16
     )
-
 
 def solution(mesh):
     placed = (

time: 723 us -> 177 us (0.24)
  blocking collectives: 517 us -> 0 us
  waiting for transfers between devices: 164 us -> 39.1 us
  starting transfers between devices: 0.09 us -> 87.4 us
    pmax x1 -> x0, blocking collectives: 257 us -> none  [on_device(): cache_max = lax.pmax(block_max, 'seq')]
    psum x1 -> x0, blocking collectives: 250 us -> none  [on_device(): lax.psum((block_sum * factor, block_out * factor[..., None]), 'seq')]
    psum x2 -> x0, waiting for transfers between devices: 131 us -> none  [the longest x1 73.2 us: on_device(): lax.psum((block_sum * factor, block_out * factor[..., None]), 'seq')]
    ppermute x0 -> x17, starting transfers between devices: none -> 83.8 us  [the longest x7 37.8 us: exchange(): other = lax.ppermute(jnp.concatenate([out, flat], axis=0), 'seq', pairs)]
    reduce_scatter x1 -> x0, waiting for transfers between devices: 32.9 us -> none  [on_device(): lax.psum_scatter(jnp.einsum('rtf,fd->rtd', hidden_all, w_down, preferred_...]
    all_gather x0 -> x3, waiting for transfers between devices: none -> 16.6 us  [the longest x1 16.6 us: on_device(): w_down_all = lax.all_gather(w_down, 'head', axis=0)]
    ppermute x0 -> x17, waiting for transfers between devices: none -> 16.4 us  [the longest x7 12.9 us: exchange(): other = lax.ppermute(jnp.concatenate([out, flat], axis=0), 'seq', pairs)]
    all_gather x1 -> x0, blocking collectives: 11.2 us -> none  [on_device(): block_rows = lax.all_gather(tokens, 'head', axis=0, tiled=True)]
  transfers between devices with their start and end apart: 3 -> 21, of which waited for: 3 -> 12; matrix products, arithmetic and copies ran while one was open for 0% -> 17% of each run, Pallas kernels for 0% -> 0%
where the time goes in v3:
time: 177 us; the launch traced here: 176 us
  starting transfers between devices  87.4 us (49%)
  waiting for transfers between devices  39.1 us (22%)
  matrix products  15.7 us (9%)
  between operations  14.3 us (8%)
  local copies, waits for them, and re-layouts  13.5 us (8%)
  other arithmetic  5.67 us (3%)
    ppermute x7, starting transfers between devices, exchange(): other = lax.ppermute(jnp.concatenate([out, flat], axis=0), 'seq', pairs)  37.8 us
    ppermute x4, starting transfers between devices, seq_attend(): other = lax.ppermute(attended, 'seq', [(i, i ^ bit) for i in range(n_seq)])  26.1 us
    ppermute x6, starting transfers between devices, head_gather(): lax.ppermute(x, 'head', [(i, (i + shift) % n_head) for i in range(n_head)])  19.9 us
    all_gather x1, waiting for transfers between devices, on_device(): w_down_all = lax.all_gather(w_down, 'head', axis=0)  16.6 us
    ppermute x7, waiting for transfers between devices, exchange(): other = lax.ppermute(jnp.concatenate([out, flat], axis=0), 'seq', pairs)  12.9 us
    all_to_all x1, waiting for transfers between devices, on_device(): own_attended = lax.all_to_all(attended, 'head', 0, 2, tiled=True)  5.28 us
    dot_general x1, matrix products, on_device(): jnp.einsum('rthf,hfd->rtd', hidden, w_down_all, preferred_element_type=jn...  4.12 us
  transfers between devices with their start and end apart: 21, of which 12 were waited for; matrix products, arithmetic and copies ran while one was open for 17% of the time, Pallas kernels for 0%

profile of v3, /device:TPU:1, one launch (start us, length us, event | category | flops | bytes accessed | tf_op | source)
XLA Modules:
  0.0 175.7 jit_solution(849618266581260817)
XLA Ops:
  6.5 0.7 all-gather.6.cloned.1.call-update
  7.3 3.9 %collective-permute-start = (bf16[16,4,1024]{2,1,0:T(4,128)(2,1)}, bf16[16,4,1024]{2,1,0:T(4,128)(2,1)S(1)}, u32[]{:S(2)}, u32[]{:S(2)}) collective-permute-start(bf16[16,4,1024]{2,1,0:T(4,128)(2,1)} %param.19), channel_id=1, source_target_pairs={{0,1},{1,2},{2,3},{3,0},{4,5},{5,6},{6,7},{7,4},{8,9},{9,10},{10,1... | collective-permute-start | bytes 393224 | tf_op jit(solution)/shard_map/ppermute | solution.py:116
  11.3 4.4 %collective-permute-start.1 = (bf16[16,4,1024]{2,1,0:T(4,128)(2,1)}, bf16[16,4,1024]{2,1,0:T(4,128)(2,1)S(1)}, u32[]{:S(2)}, u32[]{:S(2)}) collective-permute-start(bf16[16,4,1024]{2,1,0:T(4,128)(2,1)} %param.19), channel_id=1, source_target_pairs={{0,2},{1,3},{2,0},{3,1},{4,6},{5,7},{6,4},{7,5},{8,10},{9,11},{10,... | collective-permute-start | bytes 393224 | tf_op jit(solution)/shard_map/ppermute | solution.py:116
  15.6 3.1 %collective-permute-start.2 = (bf16[16,4,1024]{2,1,0:T(4,128)(2,1)}, bf16[16,4,1024]{2,1,0:T(4,128)(2,1)S(1)}, u32[]{:S(2)}, u32[]{:S(2)}) collective-permute-start(bf16[16,4,1024]{2,1,0:T(4,128)(2,1)} %param.19), channel_id=1, source_target_pairs={{0,3},{1,0},{2,1},{3,2},{4,7},{5,4},{6,5},{7,6},{8,11},{9,8},{10,9... | collective-permute-start | bytes 393224 | tf_op jit(solution)/shard_map/ppermute | solution.py:116
  18.8 0.7 broadcast_subtract_fusion
  19.6 0.2 fusion.64
  19.8 0.7 slice_bitcast_fusion
  20.5 0.7 broadcast_compare_fusion
  21.2 1.4 fusion.7
  22.6 1.9 %fusion = bf16[64,32,128]{2,1,0:T(8,128)(2,1)S(1)} fusion(bf16[64,32,128]{2,1,0:T(8,128)(2,1)} %param.20, pred[64,32]{1,0:T(8,128)(4,1)S(1)} %fusion.64, bf16[64,4,128]{2,0,1:T(8,128)(2,1)S(1)} %fusion.7, s32[64,4]{1,0:T(8,128)S(1)} %copy.293), kind=kOutput, calls=%fused_computation.3 | convolution fusion | flops 2629632 | bytes 1117184 | tf_op jit(solution)/shard_map/rjp,rjc->rpc/dot_general | solution.py:168
  24.5 0.7 compare_and_fusion
  25.2 0.4 reshape.305
  25.8 0.4 reshape.308
  26.2 0.5 pad_maximum_fusion
  26.7 1.0 gather_fusion
  27.7 1.6 fusion.6
  29.7 0.3 fusion.62
  30.0 0.1 copy.305
  30.3 0.8 select_reduce_fusion
  31.2 0.4 convert_reduce_fusion
  32.5 0.5 convolution_bitcast_fusion.2
  33.0 0.1 copy.301
  33.1 0.2 reshape.309
  33.3 0.2 copy.311
  33.6 0.3 convolution_bitcast_fusion.1
  33.9 0.1 copy.312
  34.0 0.2 reshape.315
  34.2 0.1 copy.317
  34.6 6.4 %collective-permute-start.3 = (f32[264,128]{1,0:T(8,128)S(1)}, f32[264,128]{1,0:T(8,128)S(1)}, u32[]{:S(2)}, u32[]{:S(2)}) collective-permute-start(f32[264,128]{1,0:T(8,128)S(1)} %pad_maximum_fusion.1), channel_id=1, source_target_pairs={{0,4},{4,0},{8,12},{12,8},{16,20},{20,16},{24,28},{28,24},{32,36},... | collective-permute-start | bytes 405512 | tf_op jit(solution)/shard_map/ppermute | solution.py:63
  41.0 0.9 collective-permute-done.3
  43.0 1.9 %collective-permute-start.4 = (f32[132,128]{1,0:T(8,128)S(1)}, f32[132,128]{1,0:T(8,128)S(1)}, u32[]{:S(2)}, u32[]{:S(2)}) collective-permute-start(f32[132,128]{1,0:T(8,128)S(1)} %pad_maximum_fusion.2), channel_id=1, source_target_pairs={{0,8},{4,12},{8,0},{12,4},{16,24},{20,28},{24,16},{28,20},{32,40},... | collective-permute-start | bytes 202760 | tf_op jit(solution)/shard_map/ppermute | solution.py:63
  44.9 3.1 %collective-permute-done.4 = f32[132,128]{1,0:T(8,128)S(1)} collective-permute-done((f32[132,128]{1,0:T(8,128)S(1)}, f32[132,128]{1,0:T(8,128)S(1)}, u32[]{:S(2)}, u32[]{:S(2)}) %collective-permute-start.4) | collective-permute-done | bytes 67616 | tf_op jit(solution)/shard_map/ppermute | solution.py:63
  49.0 2.6 %collective-permute-start.5 = (f32[66,128]{1,0:T(8,128)S(1)}, f32[66,128]{1,0:T(8,128)S(1)}, u32[]{:S(2)}, u32[]{:S(2)}) collective-permute-start(f32[66,128]{1,0:T(8,128)S(1)} %pad_maximum_fusion.3), channel_id=1, source_target_pairs={{0,16},{4,20},{8,24},{12,28},{16,0},{20,4},{24,8},{28,12},{32,48},... | collective-permute-start | bytes 101384 | tf_op jit(solution)/shard_map/ppermute | solution.py:63
  51.7 3.3 %collective-permute-done.5 = f32[66,128]{1,0:T(8,128)S(1)} collective-permute-done((f32[66,128]{1,0:T(8,128)S(1)}, f32[66,128]{1,0:T(8,128)S(1)}, u32[]{:S(2)}, u32[]{:S(2)}) %collective-permute-start.5) | collective-permute-done | bytes 33824 | tf_op jit(solution)/shard_map/ppermute | solution.py:63
  55.6 0.1 broadcast_in_dim.156
  56.5 6.7 %collective-permute-start.6 = (f32[33,128]{1,0:T(8,128)S(1)}, f32[33,128]{1,0:T(8,128)S(1)}, u32[]{:S(2)}, u32[]{:S(2)}) collective-permute-start(f32[33,128]{1,0:T(8,128)S(1)} %pad_maximum_fusion.4), channel_id=1, source_target_pairs={{0,32},{4,36},{8,40},{12,44},{16,48},{20,52},{24,56},{28,60},{32,0... | collective-permute-start | bytes 50696 | tf_op jit(solution)/shard_map/ppermute | solution.py:63
  63.3 1.7 collective-permute-done.6
  66.3 12.1 %collective-permute-start.7 = (f32[17,128]{1,0:T(8,128)S(1)}, f32[17,128]{1,0:T(8,128)S(1)}, u32[]{:S(2)}, u32[]{:S(2)}) collective-permute-start(f32[17,128]{1,0:T(8,128)S(1)} %pad_maximum_fusion.5), channel_id=1, source_target_pairs={{0,64},{4,68},{8,72},{12,76},{16,80},{20,84},{24,88},{28,92},{32,9... | collective-permute-start | bytes 26120 | tf_op jit(solution)/shard_map/ppermute | solution.py:63
  78.4 1.1 collective-permute-done.7
  80.7 3.2 %collective-permute-start.8 = (f32[17,128]{1,0:T(8,128)S(1)}, f32[17,128]{1,0:T(8,128)S(1)}, u32[]{:S(2)}, u32[]{:S(2)}) collective-permute-start(f32[17,128]{1,0:T(8,128)S(1)} %pad_maximum_fusion.6), channel_id=1, source_target_pairs={{0,128},{4,132},{8,136},{12,140},{16,144},{20,148},{24,152},{28,15... | collective-permute-start | bytes 26120 | tf_op jit(solution)/shard_map/ppermute | solution.py:63
  83.9 1.6 collective-permute-done.8
  86.6 4.8 %collective-permute-start.9 = (f32[17,128]{1,0:T(8,128)S(1)}, f32[17,128]{1,0:T(8,128)S(1)}, u32[]{:S(2)}, u32[]{:S(2)}) collective-permute-start(f32[17,128]{1,0:T(8,128)S(1)} %pad_maximum_fusion.7), channel_id=1, source_target_pairs={{0,256},{4,260},{8,264},{12,268},{16,272},{20,276},{24,280},{28,28... | collective-permute-start | bytes 26120 | tf_op jit(solution)/shard_map/ppermute | solution.py:63
  91.5 1.2 collective-permute-done.9
  93.8 12.1 %collective-permute-start.10 = (bf16[16,128]{1,0:T(8,128)(2,1)S(1)}, bf16[16,128]{1,0:T(8,128)(2,1)S(1)}, u32[]{:S(2)}, u32[]{:S(2)}) collective-permute-start(bf16[16,128]{1,0:T(8,128)(2,1)S(1)} %fusion.84), channel_id=1, source_target_pairs={{0,64},{4,68},{8,72},{12,76},{16,80},{20,84},{24,88},{28,92},{32,9... | collective-permute-start | bytes 12296 | tf_op jit(solution)/shard_map/ppermute | solution.py:102
  105.8 1.0 collective-permute-done.10
  106.8 7.0 %collective-permute-start.11 = (bf16[32,128]{1,0:T(8,128)(2,1)S(1)}, bf16[32,128]{1,0:T(8,128)(2,1)S(1)}, u32[]{:S(2)}, u32[]{:S(2)}) collective-permute-start(bf16[32,128]{1,0:T(8,128)(2,1)S(1)} %maximum_select_fusion.3), channel_id=1, source_target_pairs={{0,32},{4,36},{8,40},{12,44},{16,48},{20,52},{24,56},{28,60},{32,0... | collective-permute-start | bytes 24584 | tf_op jit(solution)/shard_map/ppermute | solution.py:102
  113.9 1.3 collective-permute-done.11
  115.1 3.8 %collective-permute-start.12 = (bf16[64,128]{1,0:T(8,128)(2,1)S(1)}, bf16[64,128]{1,0:T(8,128)(2,1)S(1)}, u32[]{:S(2)}, u32[]{:S(2)}) collective-permute-start(bf16[64,128]{1,0:T(8,128)(2,1)S(1)} %maximum_select_fusion.2), channel_id=1, source_target_pairs={{0,16},{4,20},{8,24},{12,28},{16,0},{20,4},{24,8},{28,12},{32,48},... | collective-permute-start | bytes 49160 | tf_op jit(solution)/shard_map/ppermute | solution.py:102
  119.0 2.2 %collective-permute-start.14 = (f32[512]{0:T(512)S(1)}, f32[512]{0:T(512)S(1)}, u32[]{:S(2)}, u32[]{:S(2)}) collective-permute-start(f32[512]{0:T(512)S(1)} %copy-done.5), channel_id=1, source_target_pairs={{0,1},{1,2},{2,3},{3,0},{4,5},{5,6},{6,7},{7,4},{8,9},{9,10},{10,1... | collective-permute-start | bytes 6152 | tf_op jit(solution)/shard_map/ppermute | solution.py:116
  121.2 2.6 %collective-permute-start.15 = (f32[512]{0:T(512)S(1)}, f32[512]{0:T(512)S(1)}, u32[]{:S(2)}, u32[]{:S(2)}) collective-permute-start(f32[512]{0:T(512)S(1)} %copy-done.5), channel_id=1, source_target_pairs={{0,2},{1,3},{2,0},{3,1},{4,6},{5,7},{6,4},{7,5},{8,10},{9,11},{10,... | collective-permute-start | bytes 6152 | tf_op jit(solution)/shard_map/ppermute | solution.py:116
  123.8 3.8 %collective-permute-start.16 = (f32[512]{0:T(512)S(1)}, f32[512]{0:T(512)S(1)}, u32[]{:S(2)}, u32[]{:S(2)}) collective-permute-start(f32[512]{0:T(512)S(1)} %copy-done.5), channel_id=1, source_target_pairs={{0,3},{1,0},{2,1},{3,2},{4,7},{5,4},{6,5},{7,6},{8,11},{9,8},{10,9... | collective-permute-start | bytes 6152 | tf_op jit(solution)/shard_map/ppermute | solution.py:116
  127.6 3.1 %collective-permute-start.13 = (bf16[128,128]{1,0:T(8,128)(2,1)S(1)}, bf16[128,128]{1,0:T(8,128)(2,1)S(1)}, u32[]{:S(2)}, u32[]{:S(2)}) collective-permute-start(bf16[128,128]{1,0:T(8,128)(2,1)S(1)} %maximum_select_fusion.1), channel_id=1, source_target_pairs={{0,8},{4,12},{8,0},{12,4},{16,24},{20,28},{24,16},{28,20},{32,40},... | collective-permute-start | bytes 98312 | tf_op jit(solution)/shard_map/ppermute | solution.py:102
  130.8 0.6 gather_fusion.1
  131.4 1.3 collective-permute-done.13
  132.7 0.6 maximum_select_fusion
  133.3 3.5 %all-to-all-start = ((bf16[64,4,128]{2,1,0:T(4,128)(2,1)}), bf16[64,4,128]{2,1,0:T(4,128)(2,1)S(1)}, u32[]{:S(2)}, u32[]{:S(2)}) async-start(bf16[64,4,128]{2,1,0:T(4,128)(2,1)} %bitcast.25), calls=%async_computation | async-start | bytes 131072 | tf_op jit(solution)/shard_map/all_to_all | solution.py:194
  136.9 5.3 %all-to-all-done = bf16[64,4,128]{2,1,0:T(4,128)(2,1)S(1)} async-done(((bf16[64,4,128]{2,1,0:T(4,128)(2,1)}), bf16[64,4,128]{2,1,0:T(4,128)(2,1)S(1)}, u32[]{:S(2)}, u32[]{:S(2)}) %all-to-all-start) | async-done | bytes 65568 | tf_op jit(solution)/shard_map/all_to_all | solution.py:194
  142.2 1.6 fusion.147
  143.8 0.2 multiply_reduce_fusion.1
  144.1 3.3 %fusion.66 = (u8[16,4,512]{2,0,1:T(8,128)(4,1)S(1)}, u8[16,4,512]{2,0,1:T(8,128)(4,1)S(1)}, f32[16,4,4,512]{3,0,2,1:T(8,128)S(1)}) fusion(f32[4,512]{1,0:T(4,128)S(1)} %broadcast_select_fusion, bf16[4,1024,512,1]{2,1,0,3:T(8,128)(2,1)} %bitcast.129, f32[1024]{0:T(1024)S(1)} %copy-done.7, f32[1024]{0:T(1024)S(1)} %copy-done.8, ...), kind=kOutput, calls=%fused_computation.103 | convolution fusion | flops 270532608 | bytes 5063168 | tf_op jit(solution)/shard_map/rtd,hdf->rthf/dot_general | solution.py:202
  147.3 16.6 %all-gather.10.cloned.1.call-done = bf16[2048,1024]{1,0:T(8,128)(2,1)} async-done(((bf16[512,1024]{1,0:T(8,128)(2,1)}), bf16[2048,1024]{1,0:T(8,128)(2,1)}) %all-gather.10.cloned.1.call-update) | async-done | bytes 4194320 | tf_op jit(solution)/shard_map/all_gather | solution.py:193
  163.9 4.1 %fusion.148 = (f32[16,4]{0,1:T(4,128)S(1)}, f32[16,4,1024]{2,0,1:T(8,128)S(1)}) fusion(f32[1024]{0:T(1024)S(1)} %copy-done.6, bf16[4,512,1024,1]{2,1,0,3:T(8,128)(2,1)} %bitcast.130, f32[16,4,4,512]{3,0,2,1:T(8,128)S(1)} %get-tuple-element.61, u8[16,4,512]{2,0,1:T(8,128)(4,1)S(1)} %get-tuple-element.6, u8[16,4,512]{2,0,1:T(8,128)(4,1)S(1)} %get-tuple-element.5, ...), kind=kOutput, calls=%fused_computation.272 | convolution fusion | flops 278200256 | bytes 5321472 | tf_op jit(solution)/shard_map/rthf,hfd->rtd/dot_general | solution.py:206
  168.1 0.2 multiply_reduce_fusion
  168.4 0.8 copy.355
  (204 shorter events, 10.1 us)
Async XLA Ops:
  6.5 19.7 %copy-start.1 = (bf16[16,4,1024]{2,1,0:T(4,128)(2,1)S(1)}, bf16[16,4,1024]{2,1,0:T(4,128)(2,1)}, u32[]{:S(2)}) copy-start(bf16[16,4,1024]{2,1,0:T(4,128)(2,1)} %param.19) | copy-start | bytes 393220
  6.5 19.2 %copy-start = (bf16[64,32,128]{2,1,0:T(8,128)(2,1)S(1)}, bf16[64,32,128]{2,1,0:T(8,128)(2,1)}, u32[]{:S(2)}) copy-start(bf16[64,32,128]{2,1,0:T(8,128)(2,1)} %param.21) | copy-start | bytes 1572868
  6.5 135.7 %all-gather.6.cloned.1.call-start = ((), (), s32[]{:S(2)}) async-start(), calls=%async_computation.1 | async-start | bytes 1310720 | tf_op jit(solution)/shard_map/all_gather | solution.py:190
  7.3 136.8 %all-gather.8.cloned.1.call-start = ((), (), s32[]{:S(2)}) async-start(), calls=%async_computation.2 | async-start | bytes 5242880 | tf_op jit(solution)/shard_map/all_gather | solution.py:191
  7.3 18.9 %collective-permute-start = (bf16[16,4,1024]{2,1,0:T(4,128)(2,1)}, bf16[16,4,1024]{2,1,0:T(4,128)(2,1)S(1)}, u32[]{:S(2)}, u32[]{:S(2)}) collective-permute-start(bf16[16,4,1024]{2,1,0:T(4,128)(2,1)} %param.19), channel_id=1, source_target_pairs={{0,1},{1,2},{2,3},{3,0},{4,5},{5,6},{6,7},{7,4},{8,9},{9,10},{10,1... | collective-permute-start | bytes 393224 | tf_op jit(solution)/shard_map/ppermute | solution.py:116
  11.3 15.0 %collective-permute-start.1 = (bf16[16,4,1024]{2,1,0:T(4,128)(2,1)}, bf16[16,4,1024]{2,1,0:T(4,128)(2,1)S(1)}, u32[]{:S(2)}, u32[]{:S(2)}) collective-permute-start(bf16[16,4,1024]{2,1,0:T(4,128)(2,1)} %param.19), channel_id=1, source_target_pairs={{0,2},{1,3},{2,0},{3,1},{4,6},{5,7},{6,4},{7,5},{8,10},{9,11},{10,... | collective-permute-start | bytes 393224 | tf_op jit(solution)/shard_map/ppermute | solution.py:116
  15.6 10.6 %collective-permute-start.2 = (bf16[16,4,1024]{2,1,0:T(4,128)(2,1)}, bf16[16,4,1024]{2,1,0:T(4,128)(2,1)S(1)}, u32[]{:S(2)}, u32[]{:S(2)}) collective-permute-start(bf16[16,4,1024]{2,1,0:T(4,128)(2,1)} %param.19), channel_id=1, source_target_pairs={{0,3},{1,0},{2,1},{3,2},{4,7},{5,4},{6,5},{7,6},{8,11},{9,8},{10,9... | collective-permute-start | bytes 393224 | tf_op jit(solution)/shard_map/ppermute | solution.py:116
  18.7 9.0 %copy-start.9 = (f32[3,128]{1,0:T(4,128)S(1)}, f32[3,128]{1,0:T(4,128)}, u32[]{:S(2)}) copy-start(f32[3,128]{1,0:T(4,128)} %param.27) | copy-start | bytes 4612
  18.7 145.2 %all-gather.10.cloned.1.call-start = ((), (), s32[]{:S(2)}) async-start(), calls=%async_computation.3 | async-start | bytes 5242880 | tf_op jit(solution)/shard_map/all_gather | solution.py:193
  34.5 84.5 %copy-start.5 = (f32[512]{0:T(512)S(1)}, f32[512]{0:T(512)}, u32[]{:S(2)}) copy-start(f32[512]{0:T(512)} %param.33) | copy-start | bytes 6148
  34.6 7.4 %collective-permute-start.3 = (f32[264,128]{1,0:T(8,128)S(1)}, f32[264,128]{1,0:T(8,128)S(1)}, u32[]{:S(2)}, u32[]{:S(2)}) collective-permute-start(f32[264,128]{1,0:T(8,128)S(1)} %pad_maximum_fusion.1), channel_id=1, source_target_pairs={{0,4},{4,0},{8,12},{12,8},{16,20},{20,16},{24,28},{28,24},{32,36},... | collective-permute-start | bytes 405512 | tf_op jit(solution)/shard_map/ppermute | solution.py:63
  42.1 100.1 %copy-start.2 = (f32[1024]{0:T(1024)S(1)}, f32[1024]{0:T(1024)}, u32[]{:S(2)}) copy-start(f32[1024]{0:T(1024)} %param.29) | copy-start | bytes 12292
  42.9 101.2 %copy-start.7 = (f32[1024]{0:T(1024)S(1)}, f32[1024]{0:T(1024)}, u32[]{:S(2)}) copy-start(f32[1024]{0:T(1024)} %param.31) | copy-start | bytes 12292
  42.9 101.2 %copy-start.8 = (f32[1024]{0:T(1024)S(1)}, f32[1024]{0:T(1024)}, u32[]{:S(2)}) copy-start(f32[1024]{0:T(1024)} %param.30) | copy-start | bytes 12292
  43.0 5.1 %collective-permute-start.4 = (f32[132,128]{1,0:T(8,128)S(1)}, f32[132,128]{1,0:T(8,128)S(1)}, u32[]{:S(2)}, u32[]{:S(2)}) collective-permute-start(f32[132,128]{1,0:T(8,128)S(1)} %pad_maximum_fusion.2), channel_id=1, source_target_pairs={{0,8},{4,12},{8,0},{12,4},{16,24},{20,28},{24,16},{28,20},{32,40},... | collective-permute-start | bytes 202760 | tf_op jit(solution)/shard_map/ppermute | solution.py:63
  49.0 6.0 %collective-permute-start.5 = (f32[66,128]{1,0:T(8,128)S(1)}, f32[66,128]{1,0:T(8,128)S(1)}, u32[]{:S(2)}, u32[]{:S(2)}) collective-permute-start(f32[66,128]{1,0:T(8,128)S(1)} %pad_maximum_fusion.3), channel_id=1, source_target_pairs={{0,16},{4,20},{8,24},{12,28},{16,0},{20,4},{24,8},{28,12},{32,48},... | collective-permute-start | bytes 101384 | tf_op jit(solution)/shard_map/ppermute | solution.py:63
  56.5 8.4 %collective-permute-start.6 = (f32[33,128]{1,0:T(8,128)S(1)}, f32[33,128]{1,0:T(8,128)S(1)}, u32[]{:S(2)}, u32[]{:S(2)}) collective-permute-start(f32[33,128]{1,0:T(8,128)S(1)} %pad_maximum_fusion.4), channel_id=1, source_target_pairs={{0,32},{4,36},{8,40},{12,44},{16,48},{20,52},{24,56},{28,60},{32,0... | collective-permute-start | bytes 50696 | tf_op jit(solution)/shard_map/ppermute | solution.py:63
  66.3 13.2 %collective-permute-start.7 = (f32[17,128]{1,0:T(8,128)S(1)}, f32[17,128]{1,0:T(8,128)S(1)}, u32[]{:S(2)}, u32[]{:S(2)}) collective-permute-start(f32[17,128]{1,0:T(8,128)S(1)} %pad_maximum_fusion.5), channel_id=1, source_target_pairs={{0,64},{4,68},{8,72},{12,76},{16,80},{20,84},{24,88},{28,92},{32,9... | collective-permute-start | bytes 26120 | tf_op jit(solution)/shard_map/ppermute | solution.py:63
  80.7 4.8 %collective-permute-start.8 = (f32[17,128]{1,0:T(8,128)S(1)}, f32[17,128]{1,0:T(8,128)S(1)}, u32[]{:S(2)}, u32[]{:S(2)}) collective-permute-start(f32[17,128]{1,0:T(8,128)S(1)} %pad_maximum_fusion.6), channel_id=1, source_target_pairs={{0,128},{4,132},{8,136},{12,140},{16,144},{20,148},{24,152},{28,15... | collective-permute-start | bytes 26120 | tf_op jit(solution)/shard_map/ppermute | solution.py:63
  86.6 6.0 %collective-permute-start.9 = (f32[17,128]{1,0:T(8,128)S(1)}, f32[17,128]{1,0:T(8,128)S(1)}, u32[]{:S(2)}, u32[]{:S(2)}) collective-permute-start(f32[17,128]{1,0:T(8,128)S(1)} %pad_maximum_fusion.7), channel_id=1, source_target_pairs={{0,256},{4,260},{8,264},{12,268},{16,272},{20,276},{24,280},{28,28... | collective-permute-start | bytes 26120 | tf_op jit(solution)/shard_map/ppermute | solution.py:63
  93.8 13.1 %collective-permute-start.10 = (bf16[16,128]{1,0:T(8,128)(2,1)S(1)}, bf16[16,128]{1,0:T(8,128)(2,1)S(1)}, u32[]{:S(2)}, u32[]{:S(2)}) collective-permute-start(bf16[16,128]{1,0:T(8,128)(2,1)S(1)} %fusion.84), channel_id=1, source_target_pairs={{0,64},{4,68},{8,72},{12,76},{16,80},{20,84},{24,88},{28,92},{32,9... | collective-permute-start | bytes 12296 | tf_op jit(solution)/shard_map/ppermute | solution.py:102
  106.8 8.3 %collective-permute-start.11 = (bf16[32,128]{1,0:T(8,128)(2,1)S(1)}, bf16[32,128]{1,0:T(8,128)(2,1)S(1)}, u32[]{:S(2)}, u32[]{:S(2)}) collective-permute-start(bf16[32,128]{1,0:T(8,128)(2,1)S(1)} %maximum_select_fusion.3), channel_id=1, source_target_pairs={{0,32},{4,36},{8,40},{12,44},{16,48},{20,52},{24,56},{28,60},{32,0... | collective-permute-start | bytes 24584 | tf_op jit(solution)/shard_map/ppermute | solution.py:102
  115.1 12.5 %collective-permute-start.12 = (bf16[64,128]{1,0:T(8,128)(2,1)S(1)}, bf16[64,128]{1,0:T(8,128)(2,1)S(1)}, u32[]{:S(2)}, u32[]{:S(2)}) collective-permute-start(bf16[64,128]{1,0:T(8,128)(2,1)S(1)} %maximum_select_fusion.2), channel_id=1, source_target_pairs={{0,16},{4,20},{8,24},{12,28},{16,0},{20,4},{24,8},{28,12},{32,48},... | collective-permute-start | bytes 49160 | tf_op jit(solution)/shard_map/ppermute | solution.py:102
  119.0 11.8 %collective-permute-start.14 = (f32[512]{0:T(512)S(1)}, f32[512]{0:T(512)S(1)}, u32[]{:S(2)}, u32[]{:S(2)}) collective-permute-start(f32[512]{0:T(512)S(1)} %copy-done.5), channel_id=1, source_target_pairs={{0,1},{1,2},{2,3},{3,0},{4,5},{5,6},{6,7},{7,4},{8,9},{9,10},{10,1... | collective-permute-start | bytes 6152 | tf_op jit(solution)/shard_map/ppermute | solution.py:116
  121.2 9.6 %collective-permute-start.15 = (f32[512]{0:T(512)S(1)}, f32[512]{0:T(512)S(1)}, u32[]{:S(2)}, u32[]{:S(2)}) collective-permute-start(f32[512]{0:T(512)S(1)} %copy-done.5), channel_id=1, source_target_pairs={{0,2},{1,3},{2,0},{3,1},{4,6},{5,7},{6,4},{7,5},{8,10},{9,11},{10,... | collective-permute-start | bytes 6152 | tf_op jit(solution)/shard_map/ppermute | solution.py:116
  123.8 7.0 %collective-permute-start.16 = (f32[512]{0:T(512)S(1)}, f32[512]{0:T(512)S(1)}, u32[]{:S(2)}, u32[]{:S(2)}) collective-permute-start(f32[512]{0:T(512)S(1)} %copy-done.5), channel_id=1, source_target_pairs={{0,3},{1,0},{2,1},{3,2},{4,7},{5,4},{6,5},{7,6},{8,11},{9,8},{10,9... | collective-permute-start | bytes 6152 | tf_op jit(solution)/shard_map/ppermute | solution.py:116
  127.6 5.1 %collective-permute-start.13 = (bf16[128,128]{1,0:T(8,128)(2,1)S(1)}, bf16[128,128]{1,0:T(8,128)(2,1)S(1)}, u32[]{:S(2)}, u32[]{:S(2)}) collective-permute-start(bf16[128,128]{1,0:T(8,128)(2,1)S(1)} %maximum_select_fusion.1), channel_id=1, source_target_pairs={{0,8},{4,12},{8,0},{12,4},{16,24},{20,28},{24,16},{28,20},{32,40},... | collective-permute-start | bytes 98312 | tf_op jit(solution)/shard_map/ppermute | solution.py:102
  133.3 8.8 %all-to-all-start = ((bf16[64,4,128]{2,1,0:T(4,128)(2,1)}), bf16[64,4,128]{2,1,0:T(4,128)(2,1)S(1)}, u32[]{:S(2)}, u32[]{:S(2)}) async-start(bf16[64,4,128]{2,1,0:T(4,128)(2,1)} %bitcast.25), calls=%async_computation | async-start | bytes 131072 | tf_op jit(solution)/shard_map/all_to_all | solution.py:194
  143.8 20.1 %copy-start.6 = (f32[1024]{0:T(1024)S(1)}, f32[1024]{0:T(1024)}, u32[]{:S(2)}) copy-start(f32[1024]{0:T(1024)} %param.35) | copy-start | bytes 12292
  163.9 4.3 %copy-start.3 = (f32[1024]{0:T(1024)S(1)}, f32[1024]{0:T(1024)}, u32[]{:S(2)}) copy-start(f32[1024]{0:T(1024)} %param.37) | copy-start | bytes 12292
  163.9 4.3 %copy-start.4 = (f32[1024]{0:T(1024)S(1)}, f32[1024]{0:T(1024)}, u32[]{:S(2)}) copy-start(f32[1024]{0:T(1024)} %param.36) | copy-start | bytes 12292
Sparse Core Ops, SparseCore 0:
  9.4 35.1 all-gather.5
  46.7 58.0 all-gather.7
  106.9 57.0 all-gather.9

commit v4 on v3

--- a/solution.py
+++ b/solution.py
@@ -75,11 +75,8 @@
     me = lax.axis_index("seq")
     rows = stats[2].shape[0]
     bit = 1
-    other = exchange(stats, [(i, i ^ bit) for i in range(n_seq)])
-    stats = merge_rows(stats, other, width)
-    bit *= 2
     scatter_bits = []
-    while bit < n_seq and rows % 16 == 0 and len(scatter_bits) < 4:
+    while bit < n_seq and rows % 16 == 0 and len(scatter_bits) < 2:
         half = rows // 2
         upper = (me // bit) % 2 == 1
         low = jax.tree.map(lambda a: a[:half], stats)
@@ -188,9 +185,15 @@
     stats = pick(first, merge_rows(cache_part, new_part, HDIM), cache_part)
     attended = seq_attend(stats, HDIM).reshape(requests, steps_count, local_width)
     w_out_all = lax.all_gather(w_out, "head", axis=0, tiled=True)
-    w_up_all = lax.all_gather(w_up, "head", axis=0)
-    up_bias_all = head_gather(up_bias)
-    w_down_all = lax.all_gather(w_down, "head", axis=0)
+    core = lax.axis_index("seq") % 2
+    ffw_half = w_up.shape[1] // 2
+    w_up_all = lax.all_gather(
+        lax.dynamic_slice_in_dim(w_up, core * ffw_half, ffw_half, 1), "head", axis=0
+    )
+    up_bias_all = head_gather(lax.dynamic_slice_in_dim(up_bias, core * ffw_half, ffw_half, 0))
+    w_down_all = lax.all_gather(
+        lax.dynamic_slice_in_dim(w_down, core * ffw_half, ffw_half, 0), "head", axis=0
+    )
     own_attended = lax.all_to_all(attended, "head", 0, 2, tiled=True)
     projected = jnp.einsum(
         "rtc,cd->rtd", own_attended, w_out_all, preferred_element_type=jnp.float32
@@ -204,6 +207,8 @@
         approximate=False,
     ).astype(jnp.bfloat16)
     lowered = jnp.einsum("rthf,hfd->rtd", hidden, w_down_all, preferred_element_type=jnp.float32)
+    n_seq = lax.axis_size("seq")
+    lowered = lowered + lax.ppermute(lowered, "seq", [(i, i ^ 1) for i in range(n_seq)])
     return layer_norm(normed.astype(jnp.float32) + lowered + down_bias, ffn_gain, ffn_shift).astype(
         jnp.bfloat16
     )

time: 177 us -> 154 us (0.87)
  waiting for transfers between devices: 39.1 us -> 20.6 us
  starting transfers between devices: 87.4 us -> 76.5 us
  local copies, waits for them, and re-layouts: 13.5 us -> 20.3 us
    all_gather x2, waiting for transfers between devices: 16.6 us -> 0.04 us  [the longest x1 0.02 us: on_device(): lax.all_gather(lax.dynamic_slice_in_dim(w_up, core * ffw_half, ffw_half,...]
    ppermute x4 -> x2, starting transfers between devices: 26.1 us -> 12.1 us  [seq_attend(): other = lax.ppermute(attended, 'seq', [(i, i ^ bit) for i in range(n_seq)])]
    ppermute x0 -> x1, starting transfers between devices: none -> 3.47 us  [on_device(): lax.ppermute(lowered, 'seq', [(i, i ^ 1) for i in range(n_seq)])]
    ppermute x4 -> x2, waiting for transfers between devices: 3.53 us -> 0.23 us  [seq_attend(): other = lax.ppermute(attended, 'seq', [(i, i ^ bit) for i in range(n_seq)])]
    dot_general x2, matrix products: 1.1 us -> 3.58 us  [partial_attention(): jnp.einsum('rthe,rphe->rthp', queries, keys_here, preferred_element_type=...]
    ppermute x7, starting transfers between devices: 37.8 us -> 36 us  [exchange(): other = lax.ppermute(jnp.concatenate([out, flat], axis=0), 'seq', pairs)]
  transfers between devices with their start and end apart: 21 -> 20, of which waited for: 12 -> 10; matrix products, arithmetic and copies ran while one was open for 17% -> 24% of each run, Pallas kernels for 0% -> 0%
where the time goes in v4:
time: 154 us; the launch traced here: 153 us
  starting transfers between devices  76.5 us (50%)
  waiting for transfers between devices  20.6 us (13%)
  local copies, waits for them, and re-layouts  20.3 us (13%)
  matrix products  16.8 us (11%)
  between operations  14.3 us (9%)
  other arithmetic  4.87 us (3%)
    ppermute x7, starting transfers between devices, exchange(): other = lax.ppermute(jnp.concatenate([out, flat], axis=0), 'seq', pairs)  36 us
    ppermute x6, starting transfers between devices, head_gather(): lax.ppermute(x, 'head', [(i, (i + shift) % n_head) for i in range(n_head)])  21.5 us
    ppermute x7, waiting for transfers between devices, exchange(): other = lax.ppermute(jnp.concatenate([out, flat], axis=0), 'seq', pairs)  13.9 us
    ppermute x2, starting transfers between devices, seq_attend(): other = lax.ppermute(attended, 'seq', [(i, i ^ bit) for i in range(n_seq)])  12.1 us
    all_to_all x1, waiting for transfers between devices, on_device(): own_attended = lax.all_to_all(attended, 'head', 0, 2, tiled=True)  5.24 us
    dot_general x2, matrix products, partial_attention(): jnp.einsum('rthe,rphe->rthp', queries, keys_here, preferred_element_type=...  3.58 us
    ppermute x1, starting transfers between devices, on_device(): lax.ppermute(lowered, 'seq', [(i, i ^ 1) for i in range(n_seq)])  3.47 us
    all_to_all x1, starting transfers between devices, on_device(): own_attended = lax.all_to_all(attended, 'head', 0, 2, tiled=True)  3.29 us
  transfers between devices with their start and end apart: 20, of which 10 were waited for; matrix products, arithmetic and copies ran while one was open for 24% of the time, Pallas kernels for 0%

profile of v4, /device:TPU:1, one launch (start us, length us, event | category | flops | bytes accessed | tf_op | source)
XLA Modules:
  0.0 153.4 jit_solution(13533502295237133806)
XLA Ops:
  6.5 4.1 %collective-permute-start = (bf16[16,4,1024]{2,1,0:T(4,128)(2,1)}, bf16[16,4,1024]{2,1,0:T(4,128)(2,1)S(1)}, u32[]{:S(2)}, u32[]{:S(2)}) collective-permute-start(bf16[16,4,1024]{2,1,0:T(4,128)(2,1)} %param.19), channel_id=1, source_target_pairs={{0,1},{1,2},{2,3},{3,0},{4,5},{5,6},{6,7},{7,4},{8,9},{9,10},{10,1... | collective-permute-start | bytes 393224 | tf_op jit(solution)/shard_map/ppermute | solution.py:113
  10.6 4.4 %collective-permute-start.1 = (bf16[16,4,1024]{2,1,0:T(4,128)(2,1)}, bf16[16,4,1024]{2,1,0:T(4,128)(2,1)S(1)}, u32[]{:S(2)}, u32[]{:S(2)}) collective-permute-start(bf16[16,4,1024]{2,1,0:T(4,128)(2,1)} %param.19), channel_id=1, source_target_pairs={{0,2},{1,3},{2,0},{3,1},{4,6},{5,7},{6,4},{7,5},{8,10},{9,11},{10,... | collective-permute-start | bytes 393224 | tf_op jit(solution)/shard_map/ppermute | solution.py:113
  15.0 3.1 %collective-permute-start.2 = (bf16[16,4,1024]{2,1,0:T(4,128)(2,1)}, bf16[16,4,1024]{2,1,0:T(4,128)(2,1)S(1)}, u32[]{:S(2)}, u32[]{:S(2)}) collective-permute-start(bf16[16,4,1024]{2,1,0:T(4,128)(2,1)} %param.19), channel_id=1, source_target_pairs={{0,3},{1,0},{2,1},{3,2},{4,7},{5,4},{6,5},{7,6},{8,11},{9,8},{10,9... | collective-permute-start | bytes 393224 | tf_op jit(solution)/shard_map/ppermute | solution.py:113
  18.2 0.7 broadcast_subtract_fusion
  19.0 0.2 fusion.61
  19.2 0.7 slice_bitcast_fusion
  19.9 0.7 broadcast_compare_fusion
  20.6 1.4 fusion.5
  22.0 1.9 %fusion = bf16[64,32,128]{2,1,0:T(8,128)(2,1)S(1)} fusion(bf16[64,32,128]{2,1,0:T(8,128)(2,1)} %param.20, pred[64,32]{1,0:T(8,128)(4,1)S(1)} %fusion.61, bf16[64,4,128]{2,0,1:T(8,128)(2,1)S(1)} %fusion.5, s32[64,4]{1,0:T(8,128)S(1)} %copy.202), kind=kOutput, calls=%fused_computation.3 | convolution fusion | flops 2629632 | bytes 1117184 | tf_op jit(solution)/shard_map/rjp,rjc->rpc/dot_general | solution.py:165
  24.0 1.4 reshape.284
  25.6 0.4 reshape.287
  26.1 0.5 pad_maximum_fusion
  26.6 1.8 %gather_fusion = bf16[4,16,4,1024]{3,2,1,0:T(4,128)(2,1)} fusion(bf16[4,16,4,1024]{3,2,1,0:T(4,128)(2,1)S(1)} %pad_maximum_fusion, s32[1024]{0:T(1024)S(1)} %pad_clamp_fusion), kind=kCustom, calls=%fused_computation | custom fusion | bytes 1048592 | tf_op jit(solution)/shard_map/jit(_take)/gather | solution.py:116
  28.3 1.9 %fusion.4 = bf16[4,3,8,8,128]{4,3,2,1,0:T(8,128)(2,1)S(1)} fusion(bf16[3,1024,128]{2,1,0:T(8,128)(2,1)} %param.26, bf16[64,4,1024]{2,1,0:T(4,128)(2,1)} %bitcast.103, pred[64]{0:T(512)(128)(4,1)S(1)} %broadcast_in_dim.144, f32[3,128]{1,0:T(4,128)S(1)} %copy-done.16), kind=kOutput, calls=%fused_computation.14 | convolution fusion | flops 201785344 | bytes 1508928 | tf_op jit(solution)/shard_map/rtd,kdc->rtkc/dot_general | solution.py:147
  30.3 0.8 reshape.286
  31.2 1.9 %fusion.29 = f32[64,2,4,4]{3,2,1,0:T(4,128)} fusion(bf16[64,4,2,64]{3,2,0,1:T(2,128)(2,1)S(1)} %reshape.290, bf16[64,4,2,64]{3,2,0,1:T(2,128)(2,1)} %reshape.286), kind=kOutput, calls=%fused_computation.63 | convolution fusion | flops 262144 | bytes 139264 | tf_op jit(solution)/shard_map/rthe,rphe->rthp/dot_general | solution.py:34
  33.1 1.1 copy.214
  34.5 1.7 %select_reduce_fusion = (f32[64,4,2]{1,2,0:T(2,128)S(1)}, f32[64,4,2,32]{3,1,2,0:T(4,128)S(1)}) fusion(pred[64,32]{1,0:T(8,128)(4,1)S(1)} %compare_and_fusion, bf16[64,4,2,64]{3,2,0,1:T(2,128)(2,1)} %reshape.286, bf16[64,32,2,64]{3,2,1,0:T(2,128)(2,1)S(1)} %copy-done.1), kind=kOutput, calls=%fused_computation.56 | convolution fusion | flops 2145792 | bytes 659456 | tf_op jit(solution)/shard_map/rthe,rphe->rthp/dot_general | solution.py:34
  36.2 0.7 copy-done.4
  36.8 0.4 convert_reduce_fusion
  38.1 1.4 convolution_bitcast_fusion.2
  39.5 0.1 copy.210
  39.7 0.2 reshape.288
  39.8 0.2 copy.220
  40.1 0.3 convolution_bitcast_fusion.1
  40.4 0.1 copy.221
  40.6 0.2 reshape.294
  41.1 6.4 %collective-permute-start.3 = (f32[132,128]{1,0:T(8,128)S(1)}, f32[132,128]{1,0:T(8,128)S(1)}, u32[]{:S(2)}, u32[]{:S(2)}) collective-permute-start(f32[132,128]{1,0:T(8,128)S(1)} %pad_maximum_fusion.1), channel_id=1, source_target_pairs={{0,4},{4,0},{8,12},{12,8},{16,20},{20,16},{24,28},{28,24},{32,36},... | collective-permute-start | bytes 202760 | tf_op jit(solution)/shard_map/ppermute | solution.py:63
  47.5 0.8 collective-permute-done.3
  49.3 1.9 %collective-permute-start.4 = (f32[66,128]{1,0:T(8,128)S(1)}, f32[66,128]{1,0:T(8,128)S(1)}, u32[]{:S(2)}, u32[]{:S(2)}) collective-permute-start(f32[66,128]{1,0:T(8,128)S(1)} %pad_maximum_fusion.2), channel_id=1, source_target_pairs={{0,8},{4,12},{8,0},{12,4},{16,24},{20,28},{24,16},{28,20},{32,40},... | collective-permute-start | bytes 101384 | tf_op jit(solution)/shard_map/ppermute | solution.py:63
  51.2 0.8 constant_dynamic-slice_fusion.1
  52.1 1.8 %collective-permute-done.4 = f32[66,128]{1,0:T(8,128)S(1)} collective-permute-done((f32[66,128]{1,0:T(8,128)S(1)}, f32[66,128]{1,0:T(8,128)S(1)}, u32[]{:S(2)}, u32[]{:S(2)}) %collective-permute-start.4) | collective-permute-done | bytes 33824 | tf_op jit(solution)/shard_map/ppermute | solution.py:63
  54.5 0.1 broadcast_in_dim.154
  55.3 2.5 %collective-permute-start.5 = (f32[66,128]{1,0:T(8,128)S(1)}, f32[66,128]{1,0:T(8,128)S(1)}, u32[]{:S(2)}, u32[]{:S(2)}) collective-permute-start(f32[66,128]{1,0:T(8,128)S(1)} %pad_maximum_fusion.3), channel_id=1, source_target_pairs={{0,16},{4,20},{8,24},{12,28},{16,0},{20,4},{24,8},{28,12},{32,48},... | collective-permute-start | bytes 101384 | tf_op jit(solution)/shard_map/ppermute | solution.py:63
  57.9 3.4 %collective-permute-done.5 = f32[66,128]{1,0:T(8,128)S(1)} collective-permute-done((f32[66,128]{1,0:T(8,128)S(1)}, f32[66,128]{1,0:T(8,128)S(1)}, u32[]{:S(2)}, u32[]{:S(2)}) %collective-permute-start.5) | collective-permute-done | bytes 33824 | tf_op jit(solution)/shard_map/ppermute | solution.py:63
  62.6 6.3 %collective-permute-start.6 = (f32[66,128]{1,0:T(8,128)S(1)}, f32[66,128]{1,0:T(8,128)S(1)}, u32[]{:S(2)}, u32[]{:S(2)}) collective-permute-start(f32[66,128]{1,0:T(8,128)S(1)} %pad_maximum_fusion.4), channel_id=1, source_target_pairs={{0,32},{4,36},{8,40},{12,44},{16,48},{20,52},{24,56},{28,60},{32,0... | collective-permute-start | bytes 101384 | tf_op jit(solution)/shard_map/ppermute | solution.py:63
  68.9 2.7 %collective-permute-done.6 = f32[66,128]{1,0:T(8,128)S(1)} collective-permute-done((f32[66,128]{1,0:T(8,128)S(1)}, f32[66,128]{1,0:T(8,128)S(1)}, u32[]{:S(2)}, u32[]{:S(2)}) %collective-permute-start.6) | collective-permute-done | bytes 33824 | tf_op jit(solution)/shard_map/ppermute | solution.py:63
  72.9 11.7 %collective-permute-start.7 = (f32[66,128]{1,0:T(8,128)S(1)}, f32[66,128]{1,0:T(8,128)S(1)}, u32[]{:S(2)}, u32[]{:S(2)}) collective-permute-start(f32[66,128]{1,0:T(8,128)S(1)} %pad_maximum_fusion.5), channel_id=1, source_target_pairs={{0,64},{4,68},{8,72},{12,76},{16,80},{20,84},{24,88},{28,92},{32,9... | collective-permute-start | bytes 101384 | tf_op jit(solution)/shard_map/ppermute | solution.py:63
  84.6 1.8 %collective-permute-done.7 = f32[66,128]{1,0:T(8,128)S(1)} collective-permute-done((f32[66,128]{1,0:T(8,128)S(1)}, f32[66,128]{1,0:T(8,128)S(1)}, u32[]{:S(2)}, u32[]{:S(2)}) %collective-permute-start.7) | collective-permute-done | bytes 33824 | tf_op jit(solution)/shard_map/ppermute | solution.py:63
  87.7 2.8 %collective-permute-start.8 = (f32[66,128]{1,0:T(8,128)S(1)}, f32[66,128]{1,0:T(8,128)S(1)}, u32[]{:S(2)}, u32[]{:S(2)}) collective-permute-start(f32[66,128]{1,0:T(8,128)S(1)} %pad_maximum_fusion.6), channel_id=1, source_target_pairs={{0,128},{4,132},{8,136},{12,140},{16,144},{20,148},{24,152},{28,15... | collective-permute-start | bytes 101384 | tf_op jit(solution)/shard_map/ppermute | solution.py:63
  90.5 0.8 constant_dynamic-slice_fusion
  91.4 1.5 collective-permute-done.8
  93.3 0.1 broadcast_in_dim.162
  94.1 4.4 %collective-permute-start.9 = (f32[66,128]{1,0:T(8,128)S(1)}, f32[66,128]{1,0:T(8,128)S(1)}, u32[]{:S(2)}, u32[]{:S(2)}) collective-permute-start(f32[66,128]{1,0:T(8,128)S(1)} %pad_maximum_fusion.7), channel_id=1, source_target_pairs={{0,256},{4,260},{8,264},{12,268},{16,272},{20,276},{24,280},{28,28... | collective-permute-start | bytes 101384 | tf_op jit(solution)/shard_map/ppermute | solution.py:63
  98.5 1.8 %collective-permute-done.9 = f32[66,128]{1,0:T(8,128)S(1)} collective-permute-done((f32[66,128]{1,0:T(8,128)S(1)}, f32[66,128]{1,0:T(8,128)S(1)}, u32[]{:S(2)}, u32[]{:S(2)}) %collective-permute-start.9) | collective-permute-done | bytes 33824 | tf_op jit(solution)/shard_map/ppermute | solution.py:63
  101.7 2.3 %collective-permute-start.10 = (bf16[64,128]{1,0:T(8,128)(2,1)S(1)}, bf16[64,128]{1,0:T(8,128)(2,1)S(1)}, u32[]{:S(2)}, u32[]{:S(2)}) collective-permute-start(bf16[64,128]{1,0:T(8,128)(2,1)S(1)} %fusion.80), channel_id=1, source_target_pairs={{0,8},{4,12},{8,0},{12,4},{16,24},{20,28},{24,16},{28,20},{32,40},... | collective-permute-start | bytes 49160 | tf_op jit(solution)/shard_map/ppermute | solution.py:99
  104.1 2.2 %collective-permute-start.12 = (f32[256]{0:T(256)S(1)}, f32[256]{0:T(256)S(1)}, u32[]{:S(2)}, u32[]{:S(2)}) collective-permute-start(f32[256]{0:T(256)S(1)} %dynamic_slice.10), channel_id=1, source_target_pairs={{0,1},{1,2},{2,3},{3,0},{4,5},{5,6},{6,7},{7,4},{8,9},{9,10},{10,1... | collective-permute-start | bytes 3080 | tf_op jit(solution)/shard_map/ppermute | solution.py:113
  106.3 3.9 %collective-permute-start.13 = (f32[256]{0:T(256)S(1)}, f32[256]{0:T(256)S(1)}, u32[]{:S(2)}, u32[]{:S(2)}) collective-permute-start(f32[256]{0:T(256)S(1)} %dynamic_slice.10), channel_id=1, source_target_pairs={{0,2},{1,3},{2,0},{3,1},{4,6},{5,7},{6,4},{7,5},{8,10},{9,11},{10,... | collective-permute-start | bytes 3080 | tf_op jit(solution)/shard_map/ppermute | solution.py:113
  110.2 4.0 %collective-permute-start.14 = (f32[256]{0:T(256)S(1)}, f32[256]{0:T(256)S(1)}, u32[]{:S(2)}, u32[]{:S(2)}) collective-permute-start(f32[256]{0:T(256)S(1)} %dynamic_slice.10), channel_id=1, source_target_pairs={{0,3},{1,0},{2,1},{3,2},{4,7},{5,4},{6,5},{7,6},{8,11},{9,8},{10,9... | collective-permute-start | bytes 3080 | tf_op jit(solution)/shard_map/ppermute | solution.py:113
  114.2 9.8 %collective-permute-start.11 = (bf16[128,128]{1,0:T(8,128)(2,1)S(1)}, bf16[128,128]{1,0:T(8,128)(2,1)S(1)}, u32[]{:S(2)}, u32[]{:S(2)}) collective-permute-start(bf16[128,128]{1,0:T(8,128)(2,1)S(1)} %maximum_select_fusion.1), channel_id=1, source_target_pairs={{0,4},{4,0},{8,12},{12,8},{16,20},{20,16},{24,28},{28,24},{32,36},... | collective-permute-start | bytes 98312 | tf_op jit(solution)/shard_map/ppermute | solution.py:99
  124.1 0.6 gather_fusion.1
  124.7 0.2 collective-permute-done.11
  124.9 0.6 maximum_select_fusion
  125.6 3.3 %all-to-all-start = ((bf16[64,4,128]{2,1,0:T(4,128)(2,1)}), bf16[64,4,128]{2,1,0:T(4,128)(2,1)S(1)}, u32[]{:S(2)}, u32[]{:S(2)}) async-start(bf16[64,4,128]{2,1,0:T(4,128)(2,1)} %bitcast.20), calls=%async_computation | async-start | bytes 131072 | tf_op jit(solution)/shard_map/all_to_all | solution.py:197
  128.9 5.2 %all-to-all-done = bf16[64,4,128]{2,1,0:T(4,128)(2,1)S(1)} async-done(((bf16[64,4,128]{2,1,0:T(4,128)(2,1)}), bf16[64,4,128]{2,1,0:T(4,128)(2,1)S(1)}, u32[]{:S(2)}, u32[]{:S(2)}) %all-to-all-start) | async-done | bytes 65568 | tf_op jit(solution)/shard_map/all_to_all | solution.py:197
  134.2 1.6 %fusion.142 = (f32[16,4]{0,1:T(4,128)S(1)}, f32[16,4,1024]{2,0,1:T(8,128)S(1)}) fusion(f32[1024]{0:T(1024)S(1)} %copy-done.6, bf16[512,1024]{1,0:T(8,128)(2,1)} %all-gather.6.cloned.1.call-done, bf16[4,4,2,8,128]{4,3,2,1,0:T(8,128)(2,1)S(1)} %bitcast.105, bf16[16,4,1024]{2,1,0:T(4,128)(2,1)S(1)} %copy-done.3), kind=kOutput, calls=%fused_computation.254 | convolution fusion | flops 67370944 | bytes 1511680 | tf_op jit(solution)/shard_map/rtc,cd->rtd/dot_general | solution.py:198
  135.9 0.2 multiply_reduce_fusion.1
  136.1 2.2 %fusion.70 = (u8[16,4,256]{2,0,1:T(8,128)(4,1)S(1)}, u8[16,4,256]{2,0,1:T(8,128)(4,1)S(1)}, f32[16,4,4,256]{3,0,2,1:T(8,128)S(1)}) fusion(f32[4,256]{1,0:T(4,128)S(1)} %broadcast_select_fusion, bf16[4,1024,256,1]{2,1,0,3:T(8,128)(2,1)} %bitcast.115, f32[1024]{0:T(1024)S(1)} %copy-done.8, f32[1024]{0:T(1024)S(1)} %copy-done.9, ...), kind=kOutput, calls=%fused_computation.109 | convolution fusion | flops 135430144 | bytes 2667008 | tf_op jit(solution)/shard_map/rtd,hdf->rthf/dot_general | solution.py:205
  138.3 2.6 %convolution_bitcast_fusion = f32[16,4,1024]{2,0,1:T(8,128)S(1)} fusion(bf16[4,256,1024,1]{2,1,0,3:T(8,128)(2,1)} %bitcast.116, f32[16,4,4,256]{3,0,2,1:T(8,128)S(1)} %get-tuple-element.63, u8[16,4,256]{2,0,1:T(8,128)(4,1)S(1)} %get-tuple-element.6, u8[16,4,256]{2,0,1:T(8,128)(4,1)S(1)} %get-tuple-element.5), kind=kOutput, calls=%fused_computation.7 | convolution fusion | flops 138805248 | bytes 2654208 | tf_op jit(solution)/shard_map/rthf,hfd->rtd/dot_general | solution.py:209
  140.9 3.5 %collective-permute-start.15 = (f32[16,4,1024]{2,0,1:T(8,128)S(1)}, f32[16,4,1024]{2,0,1:T(8,128)S(1)}, u32[]{:S(2)}, u32[]{:S(2)}) collective-permute-start(f32[16,4,1024]{2,0,1:T(8,128)S(1)} %convolution_bitcast_fusion), channel_id=1, source_target_pairs={{0,4},{4,0},{8,12},{12,8},{16,20},{20,16},{24,28},{28,24},{32,36},... | collective-permute-start | bytes 786440 | tf_op jit(solution)/shard_map/ppermute | solution.py:211
  144.4 1.1 collective-permute-done.15
  145.5 0.2 fusion.126
  145.7 0.2 multiply_reduce_fusion
  146.1 0.8 copy.264
  (211 shorter events, 10.8 us)
Async XLA Ops:
  6.5 44.7 %copy-start = (bf16[1024,512]{1,0:T(8,128)(2,1)S(1)}, bf16[1024,512]{1,0:T(8,128)(2,1)}, u32[]{:S(2)}) copy-start(bf16[1024,512]{1,0:T(8,128)(2,1)} %param.32) | copy-start | bytes 3145732
  6.5 17.4 %copy-start.12 = (s32[64]{0:T(128)S(1)}, s32[64]{0:T(128)}, u32[]{:S(2)}) copy-start(s32[64]{0:T(128)} %param.24) | copy-start | bytes 772
  6.5 127.7 %all-gather.6.cloned.1.call-start = ((), (), s32[]{:S(2)}) async-start(), calls=%async_computation.1 | async-start | bytes 1310720 | tf_op jit(solution)/shard_map/all_gather | solution.py:187
  6.5 19.5 %collective-permute-start = (bf16[16,4,1024]{2,1,0:T(4,128)(2,1)}, bf16[16,4,1024]{2,1,0:T(4,128)(2,1)S(1)}, u32[]{:S(2)}, u32[]{:S(2)}) collective-permute-start(bf16[16,4,1024]{2,1,0:T(4,128)(2,1)} %param.19), channel_id=1, source_target_pairs={{0,1},{1,2},{2,3},{3,0},{4,5},{5,6},{6,7},{7,4},{8,9},{9,10},{10,1... | collective-permute-start | bytes 393224 | tf_op jit(solution)/shard_map/ppermute | solution.py:113
  10.6 15.4 %collective-permute-start.1 = (bf16[16,4,1024]{2,1,0:T(4,128)(2,1)}, bf16[16,4,1024]{2,1,0:T(4,128)(2,1)S(1)}, u32[]{:S(2)}, u32[]{:S(2)}) collective-permute-start(bf16[16,4,1024]{2,1,0:T(4,128)(2,1)} %param.19), channel_id=1, source_target_pairs={{0,2},{1,3},{2,0},{3,1},{4,6},{5,7},{6,4},{7,5},{8,10},{9,11},{10,... | collective-permute-start | bytes 393224 | tf_op jit(solution)/shard_map/ppermute | solution.py:113
  15.0 11.1 %collective-permute-start.2 = (bf16[16,4,1024]{2,1,0:T(4,128)(2,1)}, bf16[16,4,1024]{2,1,0:T(4,128)(2,1)S(1)}, u32[]{:S(2)}, u32[]{:S(2)}) collective-permute-start(bf16[16,4,1024]{2,1,0:T(4,128)(2,1)} %param.19), channel_id=1, source_target_pairs={{0,3},{1,0},{2,1},{3,2},{4,7},{5,4},{6,5},{7,6},{8,11},{9,8},{10,9... | collective-permute-start | bytes 393224 | tf_op jit(solution)/shard_map/ppermute | solution.py:113
  18.1 118.0 %all-gather.8.cloned.1.call-start = ((), (), s32[]{:S(2)}) async-start(), calls=%async_computation.2 | async-start | bytes 2621440 | tf_op jit(solution)/shard_map/all_gather | solution.py:190
  18.2 7.4 %copy-start.13 = (pred[4]{0:T(512)(128)(4,1)}, pred[4]{0:T(512)(128)(4,1)S(1)}, u32[]{:S(2)}) copy-start(pred[4]{0:T(512)(128)(4,1)S(1)} %compare_and_fusion.1) | copy-start | bytes 16
  18.2 7.4 %copy-start.2 = (bf16[64,32,128]{2,1,0:T(8,128)(2,1)S(1)}, bf16[64,32,128]{2,1,0:T(8,128)(2,1)}, u32[]{:S(2)}) copy-start(bf16[64,32,128]{2,1,0:T(8,128)(2,1)} %param.21) | copy-start | bytes 1572868
  22.0 4.1 %copy-start.3 = (bf16[16,4,1024]{2,1,0:T(4,128)(2,1)S(1)}, bf16[16,4,1024]{2,1,0:T(4,128)(2,1)}, u32[]{:S(2)}) copy-start(bf16[16,4,1024]{2,1,0:T(4,128)(2,1)} %param.19) | copy-start | bytes 393220
  25.4 2.9 %copy-start.16 = (f32[3,128]{1,0:T(4,128)S(1)}, f32[3,128]{1,0:T(4,128)}, u32[]{:S(2)}) copy-start(f32[3,128]{1,0:T(4,128)} %param.27) | copy-start | bytes 4612
  28.3 6.1 %copy-start.1 = (bf16[64,32,2,64]{3,2,1,0:T(2,128)(2,1)S(1)}, bf16[64,32,2,64]{3,2,1,0:T(2,128)(2,1)}, u32[]{:S(2)}) copy-start(bf16[64,32,2,64]{3,2,1,0:T(2,128)(2,1)} %reshape.284) | copy-start | bytes 1572868
  36.2 0.7 copy-start.4
  41.1 7.3 %collective-permute-start.3 = (f32[132,128]{1,0:T(8,128)S(1)}, f32[132,128]{1,0:T(8,128)S(1)}, u32[]{:S(2)}, u32[]{:S(2)}) collective-permute-start(f32[132,128]{1,0:T(8,128)S(1)} %pad_maximum_fusion.1), channel_id=1, source_target_pairs={{0,4},{4,0},{8,12},{12,8},{16,20},{20,16},{24,28},{28,24},{32,36},... | collective-permute-start | bytes 202760 | tf_op jit(solution)/shard_map/ppermute | solution.py:63
  49.3 4.7 %collective-permute-start.4 = (f32[66,128]{1,0:T(8,128)S(1)}, f32[66,128]{1,0:T(8,128)S(1)}, u32[]{:S(2)}, u32[]{:S(2)}) collective-permute-start(f32[66,128]{1,0:T(8,128)S(1)} %pad_maximum_fusion.2), channel_id=1, source_target_pairs={{0,8},{4,12},{8,0},{12,4},{16,24},{20,28},{24,16},{28,20},{32,40},... | collective-permute-start | bytes 101384 | tf_op jit(solution)/shard_map/ppermute | solution.py:63
  52.1 38.4 %copy-start.5 = (bf16[512,1024]{1,0:T(8,128)(2,1)S(1)}, bf16[512,1024]{1,0:T(8,128)(2,1)}, u32[]{:S(2)}) copy-start(bf16[512,1024]{1,0:T(8,128)(2,1)} %param.34) | copy-start | bytes 3145732
  52.1 86.2 %all-gather.10.cloned.1.call-start = ((), (), s32[]{:S(2)}) async-start(), calls=%async_computation.3 | async-start | bytes 2621440 | tf_op jit(solution)/shard_map/all_gather | solution.py:194
  55.3 6.0 %collective-permute-start.5 = (f32[66,128]{1,0:T(8,128)S(1)}, f32[66,128]{1,0:T(8,128)S(1)}, u32[]{:S(2)}, u32[]{:S(2)}) collective-permute-start(f32[66,128]{1,0:T(8,128)S(1)} %pad_maximum_fusion.3), channel_id=1, source_target_pairs={{0,16},{4,20},{8,24},{12,28},{16,0},{20,4},{24,8},{28,12},{32,48},... | collective-permute-start | bytes 101384 | tf_op jit(solution)/shard_map/ppermute | solution.py:63
  62.6 9.0 %collective-permute-start.6 = (f32[66,128]{1,0:T(8,128)S(1)}, f32[66,128]{1,0:T(8,128)S(1)}, u32[]{:S(2)}, u32[]{:S(2)}) collective-permute-start(f32[66,128]{1,0:T(8,128)S(1)} %pad_maximum_fusion.4), channel_id=1, source_target_pairs={{0,32},{4,36},{8,40},{12,44},{16,48},{20,52},{24,56},{28,60},{32,0... | collective-permute-start | bytes 101384 | tf_op jit(solution)/shard_map/ppermute | solution.py:63
  72.9 13.5 %collective-permute-start.7 = (f32[66,128]{1,0:T(8,128)S(1)}, f32[66,128]{1,0:T(8,128)S(1)}, u32[]{:S(2)}, u32[]{:S(2)}) collective-permute-start(f32[66,128]{1,0:T(8,128)S(1)} %pad_maximum_fusion.5), channel_id=1, source_target_pairs={{0,64},{4,68},{8,72},{12,76},{16,80},{20,84},{24,88},{28,92},{32,9... | collective-permute-start | bytes 101384 | tf_op jit(solution)/shard_map/ppermute | solution.py:63
  87.2 16.8 %copy-start.15 = (f32[512]{0:T(512)S(1)}, f32[512]{0:T(512)}, u32[]{:S(2)}) copy-start(f32[512]{0:T(512)} %param.33) | copy-start | bytes 6148
  87.7 41.2 %copy-start.14 = (pred[4]{0:T(512)(128)(4,1)S(1)}, pred[4]{0:T(512)(128)(4,1)}, u32[]{:S(2)}) copy-start(pred[4]{0:T(512)(128)(4,1)} %copy-done.13) | copy-start | bytes 16
  87.7 46.5 %copy-start.6 = (f32[1024]{0:T(1024)S(1)}, f32[1024]{0:T(1024)}, u32[]{:S(2)}) copy-start(f32[1024]{0:T(1024)} %param.29) | copy-start | bytes 12292
  87.7 5.1 %collective-permute-start.8 = (f32[66,128]{1,0:T(8,128)S(1)}, f32[66,128]{1,0:T(8,128)S(1)}, u32[]{:S(2)}, u32[]{:S(2)}) collective-permute-start(f32[66,128]{1,0:T(8,128)S(1)} %pad_maximum_fusion.6), channel_id=1, source_target_pairs={{0,128},{4,132},{8,136},{12,140},{16,144},{20,148},{24,152},{28,15... | collective-permute-start | bytes 101384 | tf_op jit(solution)/shard_map/ppermute | solution.py:63
  93.3 42.8 %copy-start.8 = (f32[1024]{0:T(1024)S(1)}, f32[1024]{0:T(1024)}, u32[]{:S(2)}) copy-start(f32[1024]{0:T(1024)} %param.31) | copy-start | bytes 12292
  93.3 42.8 %copy-start.9 = (f32[1024]{0:T(1024)S(1)}, f32[1024]{0:T(1024)}, u32[]{:S(2)}) copy-start(f32[1024]{0:T(1024)} %param.30) | copy-start | bytes 12292
  94.1 6.2 %collective-permute-start.9 = (f32[66,128]{1,0:T(8,128)S(1)}, f32[66,128]{1,0:T(8,128)S(1)}, u32[]{:S(2)}, u32[]{:S(2)}) collective-permute-start(f32[66,128]{1,0:T(8,128)S(1)} %pad_maximum_fusion.7), channel_id=1, source_target_pairs={{0,256},{4,260},{8,264},{12,268},{16,272},{20,276},{24,280},{28,28... | collective-permute-start | bytes 101384 | tf_op jit(solution)/shard_map/ppermute | solution.py:63
  101.7 12.5 %collective-permute-start.10 = (bf16[64,128]{1,0:T(8,128)(2,1)S(1)}, bf16[64,128]{1,0:T(8,128)(2,1)S(1)}, u32[]{:S(2)}, u32[]{:S(2)}) collective-permute-start(bf16[64,128]{1,0:T(8,128)(2,1)S(1)} %fusion.80), channel_id=1, source_target_pairs={{0,8},{4,12},{8,0},{12,4},{16,24},{20,28},{24,16},{28,20},{32,40},... | collective-permute-start | bytes 49160 | tf_op jit(solution)/shard_map/ppermute | solution.py:99
  104.1 20.0 %collective-permute-start.12 = (f32[256]{0:T(256)S(1)}, f32[256]{0:T(256)S(1)}, u32[]{:S(2)}, u32[]{:S(2)}) collective-permute-start(f32[256]{0:T(256)S(1)} %dynamic_slice.10), channel_id=1, source_target_pairs={{0,1},{1,2},{2,3},{3,0},{4,5},{5,6},{6,7},{7,4},{8,9},{9,10},{10,1... | collective-permute-start | bytes 3080 | tf_op jit(solution)/shard_map/ppermute | solution.py:113
  106.3 17.8 %collective-permute-start.13 = (f32[256]{0:T(256)S(1)}, f32[256]{0:T(256)S(1)}, u32[]{:S(2)}, u32[]{:S(2)}) collective-permute-start(f32[256]{0:T(256)S(1)} %dynamic_slice.10), channel_id=1, source_target_pairs={{0,2},{1,3},{2,0},{3,1},{4,6},{5,7},{6,4},{7,5},{8,10},{9,11},{10,... | collective-permute-start | bytes 3080 | tf_op jit(solution)/shard_map/ppermute | solution.py:113
  110.2 13.9 %collective-permute-start.14 = (f32[256]{0:T(256)S(1)}, f32[256]{0:T(256)S(1)}, u32[]{:S(2)}, u32[]{:S(2)}) collective-permute-start(f32[256]{0:T(256)S(1)} %dynamic_slice.10), channel_id=1, source_target_pairs={{0,3},{1,0},{2,1},{3,2},{4,7},{5,4},{6,5},{7,6},{8,11},{9,8},{10,9... | collective-permute-start | bytes 3080 | tf_op jit(solution)/shard_map/ppermute | solution.py:113
  114.2 10.7 %collective-permute-start.11 = (bf16[128,128]{1,0:T(8,128)(2,1)S(1)}, bf16[128,128]{1,0:T(8,128)(2,1)S(1)}, u32[]{:S(2)}, u32[]{:S(2)}) collective-permute-start(bf16[128,128]{1,0:T(8,128)(2,1)S(1)} %maximum_select_fusion.1), channel_id=1, source_target_pairs={{0,4},{4,0},{8,12},{12,8},{16,20},{20,16},{24,28},{28,24},{32,36},... | collective-permute-start | bytes 98312 | tf_op jit(solution)/shard_map/ppermute | solution.py:99
  125.6 8.6 %all-to-all-start = ((bf16[64,4,128]{2,1,0:T(4,128)(2,1)}), bf16[64,4,128]{2,1,0:T(4,128)(2,1)S(1)}, u32[]{:S(2)}, u32[]{:S(2)}) async-start(bf16[64,4,128]{2,1,0:T(4,128)(2,1)} %bitcast.20), calls=%async_computation | async-start | bytes 131072 | tf_op jit(solution)/shard_map/all_to_all | solution.py:197
  138.3 7.2 %copy-start.7 = (f32[1024]{0:T(1024)S(1)}, f32[1024]{0:T(1024)}, u32[]{:S(2)}) copy-start(f32[1024]{0:T(1024)} %param.35) | copy-start | bytes 12292
  138.3 7.6 %copy-start.10 = (f32[1024]{0:T(1024)S(1)}, f32[1024]{0:T(1024)}, u32[]{:S(2)}) copy-start(f32[1024]{0:T(1024)} %param.37) | copy-start | bytes 12292
  138.3 7.6 %copy-start.11 = (f32[1024]{0:T(1024)S(1)}, f32[1024]{0:T(1024)}, u32[]{:S(2)}) copy-start(f32[1024]{0:T(1024)} %param.36) | copy-start | bytes 12292
  140.9 4.6 %collective-permute-start.15 = (f32[16,4,1024]{2,0,1:T(8,128)S(1)}, f32[16,4,1024]{2,0,1:T(8,128)S(1)}, u32[]{:S(2)}, u32[]{:S(2)}) collective-permute-start(f32[16,4,1024]{2,0,1:T(8,128)S(1)} %convolution_bitcast_fusion), channel_id=1, source_target_pairs={{0,4},{4,0},{8,12},{12,8},{16,20},{20,16},{24,28},{28,24},{32,36},... | collective-permute-start | bytes 786440 | tf_op jit(solution)/shard_map/ppermute | solution.py:211
Sparse Core Ops, SparseCore 0:
  18.2 32.5 all-gather.5
  52.9 40.7 all-gather.7
  95.8 38.9 all-gather.9

commit v5 on v4

--- a/solution.py
+++ b/solution.py
@@ -184,19 +184,44 @@
     first = lax.axis_index("seq") == 0
     stats = pick(first, merge_rows(cache_part, new_part, HDIM), cache_part)
     attended = seq_attend(stats, HDIM).reshape(requests, steps_count, local_width)
-    w_out_all = lax.all_gather(w_out, "head", axis=0, tiled=True)
+    n_seq = lax.axis_size("seq")
     core = lax.axis_index("seq") % 2
+    pair = [(i, i ^ 1) for i in range(n_seq)]
+    d_half = w_out.shape[1] // 2
+    w_out_all = lax.all_gather(
+        lax.dynamic_slice_in_dim(w_out, core * d_half, d_half, 1), "head", axis=0, tiled=True
+    )
     ffw_half = w_up.shape[1] // 2
+    bias_half = lax.dynamic_slice_in_dim(up_bias, core * ffw_half, ffw_half, 0)
+    bias_hi = lax.reduce_precision(bias_half, exponent_bits=8, mantissa_bits=7)
+    rest = bias_half - bias_hi
+    bias_mid = lax.reduce_precision(rest, exponent_bits=8, mantissa_bits=7)
+    bias_lo = rest - bias_mid
+    pieces = jnp.stack([bias_hi, bias_mid, bias_lo]).astype(jnp.bfloat16)
+    pieces = jnp.pad(pieces, ((0, 5), (0, 0)))
+    up_rows = w_up.shape[0]
     w_up_all = lax.all_gather(
-        lax.dynamic_slice_in_dim(w_up, core * ffw_half, ffw_half, 1), "head", axis=0
-    )
-    up_bias_all = head_gather(lax.dynamic_slice_in_dim(up_bias, core * ffw_half, ffw_half, 0))
+        jnp.concatenate(
+            [lax.dynamic_slice_in_dim(w_up, core * ffw_half, ffw_half, 1), pieces], axis=0
+        ),
+        "head",
+        axis=0,
+    )
+    got = w_up_all[:, up_rows : up_rows + 3].astype(jnp.float32)
+    up_bias_all = got[:, 0] + got[:, 1] + got[:, 2]
+    w_up_all = w_up_all[:, :up_rows]
     w_down_all = lax.all_gather(
         lax.dynamic_slice_in_dim(w_down, core * ffw_half, ffw_half, 0), "head", axis=0
     )
     own_attended = lax.all_to_all(attended, "head", 0, 2, tiled=True)
     projected = jnp.einsum(
         "rtc,cd->rtd", own_attended, w_out_all, preferred_element_type=jnp.float32
+    )
+    other_half = lax.ppermute(projected, "seq", pair)
+    projected = jnp.where(
+        core == 1,
+        jnp.concatenate([other_half, projected], axis=2),
+        jnp.concatenate([projected, other_half], axis=2),
     )
     normed = layer_norm(
         tokens.astype(jnp.float32) + projected + out_bias, attn_gain, attn_shift
@@ -207,8 +232,7 @@
         approximate=False,
     ).astype(jnp.bfloat16)
     lowered = jnp.einsum("rthf,hfd->rtd", hidden, w_down_all, preferred_element_type=jnp.float32)
-    n_seq = lax.axis_size("seq")
-    lowered = lowered + lax.ppermute(lowered, "seq", [(i, i ^ 1) for i in range(n_seq)])
+    lowered = lowered + lax.ppermute(lowered, "seq", pair)
     return layer_norm(normed.astype(jnp.float32) + lowered + down_bias, ffn_gain, ffn_shift).astype(
         jnp.bfloat16
     )

time: 154 us -> 162 us (1.052)
  blocking collectives: 0 us -> 15.3 us
  starting transfers between devices: 76.5 us -> 71.5 us
  other arithmetic: 4.87 us -> 9.36 us
  matrix products: 16.8 us -> 13 us
  waiting for transfers between devices: 20.6 us -> 16.9 us
    all_gather x0 -> x1, blocking collectives: none -> 15.3 us  [on_device(): lax.all_gather(lax.dynamic_slice_in_dim(w_out, core * d_half, d_half, 1),...]
    ppermute x6 -> x3, starting transfers between devices: 21.5 us -> 11.5 us  [head_gather(): lax.ppermute(x, 'head', [(i, (i + shift) % n_head) for i in range(n_head)])]
    all_to_all x1, waiting for transfers between devices: 5.24 us -> 0.01 us  [on_device(): own_attended = lax.all_to_all(attended, 'head', 0, 2, tiled=True)]
    ppermute x2, waiting for transfers between devices: 0.23 us -> 2.86 us  [seq_attend(): other = lax.ppermute(attended, 'seq', [(i, i ^ bit) for i in range(n_seq)])]
    ppermute x1 -> x2, starting transfers between devices: 3.47 us -> 5.59 us  [the longest x1 3.32 us: on_device(): other_half = lax.ppermute(projected, 'seq', pair)]
    ppermute x7, waiting for transfers between devices: 13.9 us -> 11.9 us  [exchange(): other = lax.ppermute(jnp.concatenate([out, flat], axis=0), 'seq', pairs)]
    another operation x0 -> x3, local copies, waits for them, and re-layouts: none -> 1.76 us  [on_device(): pieces = jnp.stack([bias_hi, bias_mid, bias_lo]).astype(jnp.bfloat16)]
  transfers between devices with their start and end apart: 20 -> 17, of which waited for: 10 -> 11; matrix products, arithmetic and copies ran while one was open for 24% -> 15% of each run, Pallas kernels for 0% -> 0%
where the time goes in v5:
time: 162 us; the launch traced here: 161 us
  starting transfers between devices  71.5 us (44%)
  local copies, waits for them, and re-layouts  20.2 us (12%)
  waiting for transfers between devices  16.9 us (10%)
  blocking collectives  15.3 us (9%)
  between operations  14.6 us (9%)
  matrix products  13 us (8%)
  other arithmetic  9.36 us (6%)
    ppermute x7, starting transfers between devices, exchange(): other = lax.ppermute(jnp.concatenate([out, flat], axis=0), 'seq', pairs)  37.4 us
    all_gather x1, blocking collectives, on_device(): lax.all_gather(lax.dynamic_slice_in_dim(w_out, core * d_half, d_half, 1),...  15.3 us
    ppermute x2, starting transfers between devices, seq_attend(): other = lax.ppermute(attended, 'seq', [(i, i ^ bit) for i in range(n_seq)])  12.5 us
    ppermute x7, waiting for transfers between devices, exchange(): other = lax.ppermute(jnp.concatenate([out, flat], axis=0), 'seq', pairs)  11.9 us
    ppermute x3, starting transfers between devices, head_gather(): lax.ppermute(x, 'head', [(i, (i + shift) % n_head) for i in range(n_head)])  11.5 us
    all_to_all x1, starting transfers between devices, on_device(): own_attended = lax.all_to_all(attended, 'head', 0, 2, tiled=True)  4.42 us
    ppermute x1, starting transfers between devices, on_device(): other_half = lax.ppermute(projected, 'seq', pair)  3.32 us
  transfers between devices with their start and end apart: 17, of which 11 were waited for; matrix products, arithmetic and copies ran while one was open for 15% of the time, Pallas kernels for 0%

profile of v5, /device:TPU:1, one launch (start us, length us, event | category | flops | bytes accessed | tf_op | source)
XLA Modules:
  0.0 160.9 jit_solution(11353133815378401334)
XLA Ops:
  6.5 4.1 %collective-permute-start = (bf16[16,4,1024]{2,1,0:T(4,128)(2,1)}, bf16[16,4,1024]{2,1,0:T(4,128)(2,1)S(1)}, u32[]{:S(2)}, u32[]{:S(2)}) collective-permute-start(bf16[16,4,1024]{2,1,0:T(4,128)(2,1)} %param.19), channel_id=1, source_target_pairs={{0,1},{1,2},{2,3},{3,0},{4,5},{5,6},{6,7},{7,4},{8,9},{9,10},{10,1... | collective-permute-start | bytes 393224 | tf_op jit(solution)/shard_map/ppermute | solution.py:113
  10.6 4.4 %collective-permute-start.1 = (bf16[16,4,1024]{2,1,0:T(4,128)(2,1)}, bf16[16,4,1024]{2,1,0:T(4,128)(2,1)S(1)}, u32[]{:S(2)}, u32[]{:S(2)}) collective-permute-start(bf16[16,4,1024]{2,1,0:T(4,128)(2,1)} %param.19), channel_id=1, source_target_pairs={{0,2},{1,3},{2,0},{3,1},{4,6},{5,7},{6,4},{7,5},{8,10},{9,11},{10,... | collective-permute-start | bytes 393224 | tf_op jit(solution)/shard_map/ppermute | solution.py:113
  15.0 3.1 %collective-permute-start.2 = (bf16[16,4,1024]{2,1,0:T(4,128)(2,1)}, bf16[16,4,1024]{2,1,0:T(4,128)(2,1)S(1)}, u32[]{:S(2)}, u32[]{:S(2)}) collective-permute-start(bf16[16,4,1024]{2,1,0:T(4,128)(2,1)} %param.19), channel_id=1, source_target_pairs={{0,3},{1,0},{2,1},{3,2},{4,7},{5,4},{6,5},{7,6},{8,11},{9,8},{10,9... | collective-permute-start | bytes 393224 | tf_op jit(solution)/shard_map/ppermute | solution.py:113
  18.1 0.7 broadcast_subtract_fusion
  19.1 0.7 slice_bitcast_fusion.4
  19.8 0.7 broadcast_compare_fusion
  20.5 0.8 reduce-precision_convert_fusion.1
  21.2 1.4 fusion.6
  22.6 1.9 %fusion.1 = bf16[64,32,128]{2,1,0:T(8,128)(2,1)S(1)} fusion(bf16[64,32,128]{2,1,0:T(8,128)(2,1)} %param.20, pred[64,32]{1,0:T(8,128)(4,1)S(1)} %fusion.65, bf16[64,4,128]{2,0,1:T(8,128)(2,1)S(1)} %fusion.6, s32[64,4]{1,0:T(8,128)S(1)} %copy.202), kind=kOutput, calls=%fused_computation.4 | convolution fusion | flops 2629632 | bytes 1117184 | tf_op jit(solution)/shard_map/rjp,rjc->rpc/dot_general | solution.py:165
  24.7 1.4 reshape.288
  26.2 0.6 broadcast_in_dim.134
  26.7 0.4 reshape.291
  27.2 0.6 stack.36
  27.7 0.6 stack.37
  28.3 0.6 stack.38
  29.0 0.6 copy-done.4
  29.7 1.4 pad_maximum_fusion.1
  31.0 1.8 %gather_fusion = bf16[4,16,4,1024]{3,2,1,0:T(4,128)(2,1)} fusion(bf16[4,16,4,1024]{3,2,1,0:T(4,128)(2,1)S(1)} %pad_maximum_fusion.1, s32[1024]{0:T(1024)S(1)} %pad_clamp_fusion), kind=kCustom, calls=%fused_computation | custom fusion | bytes 1048592 | tf_op jit(solution)/shard_map/jit(_take)/gather | solution.py:116
  32.8 1.8 %fusion.5 = bf16[4,3,8,8,128]{4,3,2,1,0:T(8,128)(2,1)S(1)} fusion(bf16[3,1024,128]{2,1,0:T(8,128)(2,1)} %param.26, bf16[64,4,1024]{2,1,0:T(4,128)(2,1)} %bitcast.103, pred[64]{0:T(512)(128)(4,1)} %broadcast_in_dim.134, f32[3,128]{1,0:T(4,128)} %param.27), kind=kOutput, calls=%fused_computation.13 | convolution fusion | flops 201785344 | bytes 1508928 | tf_op jit(solution)/shard_map/rtd,kdc->rtkc/dot_general | solution.py:147
  34.9 0.3 fusion.33
  35.5 0.7 convert_reduce_fusion.1
  36.3 2.0 %select_reduce_fusion = (f32[64,4,2]{1,2,0:T(2,128)S(1)}, f32[64,4,2,32]{3,1,2,0:T(4,128)S(1)}) fusion(pred[64,32]{1,0:T(8,128)(4,1)S(1)} %compare_and_fusion, bf16[64,4,2,64]{3,2,0,1:T(2,128)(2,1)S(1)} %reshape.290, bf16[64,32,2,64]{3,2,1,0:T(2,128)(2,1)} %reshape.288), kind=kOutput, calls=%fused_computation.60 | convolution fusion | flops 2145792 | bytes 659456 | tf_op jit(solution)/shard_map/rthe,rphe->rthp/dot_general | solution.py:34
  38.3 0.4 convert_reduce_fusion
  39.3 0.6 add_select_fusion.1
  40.0 0.7 broadcast_in_dim.141
  40.8 0.5 convolution_bitcast_fusion.2
  41.5 0.2 reshape.292
  41.9 0.3 convolution_bitcast_fusion.1
  42.4 0.2 reshape.298
  42.9 6.4 %collective-permute-start.3 = (f32[132,128]{1,0:T(8,128)S(1)}, f32[132,128]{1,0:T(8,128)S(1)}, u32[]{:S(2)}, u32[]{:S(2)}) collective-permute-start(f32[132,128]{1,0:T(8,128)S(1)} %pad_maximum_fusion.2), channel_id=1, source_target_pairs={{0,4},{4,0},{8,12},{12,8},{16,20},{20,16},{24,28},{28,24},{32,36},... | collective-permute-start | bytes 202760 | tf_op jit(solution)/shard_map/ppermute | solution.py:63
  49.3 0.8 collective-permute-done.3
  51.1 1.9 %collective-permute-start.4 = (f32[66,128]{1,0:T(8,128)S(1)}, f32[66,128]{1,0:T(8,128)S(1)}, u32[]{:S(2)}, u32[]{:S(2)}) collective-permute-start(f32[66,128]{1,0:T(8,128)S(1)} %pad_maximum_fusion.3), channel_id=1, source_target_pairs={{0,8},{4,12},{8,0},{12,4},{16,24},{20,28},{24,16},{28,20},{32,40},... | collective-permute-start | bytes 101384 | tf_op jit(solution)/shard_map/ppermute | solution.py:63
  53.1 0.9 pad_maximum_fusion
  54.0 1.8 %collective-permute-done.4 = f32[66,128]{1,0:T(8,128)S(1)} collective-permute-done((f32[66,128]{1,0:T(8,128)S(1)}, f32[66,128]{1,0:T(8,128)S(1)}, u32[]{:S(2)}, u32[]{:S(2)}) %collective-permute-start.4) | collective-permute-done | bytes 33824 | tf_op jit(solution)/shard_map/ppermute | solution.py:63
  57.2 2.1 %collective-permute-start.5 = (f32[66,128]{1,0:T(8,128)S(1)}, f32[66,128]{1,0:T(8,128)S(1)}, u32[]{:S(2)}, u32[]{:S(2)}) collective-permute-start(f32[66,128]{1,0:T(8,128)S(1)} %pad_maximum_fusion.4), channel_id=1, source_target_pairs={{0,16},{4,20},{8,24},{12,28},{16,0},{20,4},{24,8},{28,12},{32,48},... | collective-permute-start | bytes 101384 | tf_op jit(solution)/shard_map/ppermute | solution.py:63
  59.3 3.6 %collective-permute-done.5 = f32[66,128]{1,0:T(8,128)S(1)} collective-permute-done((f32[66,128]{1,0:T(8,128)S(1)}, f32[66,128]{1,0:T(8,128)S(1)}, u32[]{:S(2)}, u32[]{:S(2)}) %collective-permute-start.5) | collective-permute-done | bytes 33824 | tf_op jit(solution)/shard_map/ppermute | solution.py:63
  64.2 6.6 %collective-permute-start.6 = (f32[66,128]{1,0:T(8,128)S(1)}, f32[66,128]{1,0:T(8,128)S(1)}, u32[]{:S(2)}, u32[]{:S(2)}) collective-permute-start(f32[66,128]{1,0:T(8,128)S(1)} %pad_maximum_fusion.5), channel_id=1, source_target_pairs={{0,32},{4,36},{8,40},{12,44},{16,48},{20,52},{24,56},{28,60},{32,0... | collective-permute-start | bytes 101384 | tf_op jit(solution)/shard_map/ppermute | solution.py:63
  70.8 2.0 %collective-permute-done.6 = f32[66,128]{1,0:T(8,128)S(1)} collective-permute-done((f32[66,128]{1,0:T(8,128)S(1)}, f32[66,128]{1,0:T(8,128)S(1)}, u32[]{:S(2)}, u32[]{:S(2)}) %collective-permute-start.6) | collective-permute-done | bytes 33824 | tf_op jit(solution)/shard_map/ppermute | solution.py:63
  74.1 12.4 %collective-permute-start.7 = (f32[66,128]{1,0:T(8,128)S(1)}, f32[66,128]{1,0:T(8,128)S(1)}, u32[]{:S(2)}, u32[]{:S(2)}) collective-permute-start(f32[66,128]{1,0:T(8,128)S(1)} %pad_maximum_fusion.6), channel_id=1, source_target_pairs={{0,64},{4,68},{8,72},{12,76},{16,80},{20,84},{24,88},{28,92},{32,9... | collective-permute-start | bytes 101384 | tf_op jit(solution)/shard_map/ppermute | solution.py:63
  86.5 1.4 collective-permute-done.7
  89.1 3.2 %collective-permute-start.8 = (f32[66,128]{1,0:T(8,128)S(1)}, f32[66,128]{1,0:T(8,128)S(1)}, u32[]{:S(2)}, u32[]{:S(2)}) collective-permute-start(f32[66,128]{1,0:T(8,128)S(1)} %pad_maximum_fusion.7), channel_id=1, source_target_pairs={{0,128},{4,132},{8,136},{12,140},{16,144},{20,148},{24,152},{28,15... | collective-permute-start | bytes 101384 | tf_op jit(solution)/shard_map/ppermute | solution.py:63
  92.4 0.8 constant_dynamic-slice_fusion
  93.2 0.6 collective-permute-done.8
  95.2 4.8 %collective-permute-start.9 = (f32[66,128]{1,0:T(8,128)S(1)}, f32[66,128]{1,0:T(8,128)S(1)}, u32[]{:S(2)}, u32[]{:S(2)}) collective-permute-start(f32[66,128]{1,0:T(8,128)S(1)} %pad_maximum_fusion.8), channel_id=1, source_target_pairs={{0,256},{4,260},{8,264},{12,268},{16,272},{20,276},{24,280},{28,28... | collective-permute-start | bytes 101384 | tf_op jit(solution)/shard_map/ppermute | solution.py:63
  100.0 1.6 %collective-permute-done.9 = f32[66,128]{1,0:T(8,128)S(1)} collective-permute-done((f32[66,128]{1,0:T(8,128)S(1)}, f32[66,128]{1,0:T(8,128)S(1)}, u32[]{:S(2)}, u32[]{:S(2)}) %collective-permute-start.9) | collective-permute-done | bytes 33824 | tf_op jit(solution)/shard_map/ppermute | solution.py:63
  103.0 2.7 %collective-permute-start.10 = (bf16[64,128]{1,0:T(8,128)(2,1)S(1)}, bf16[64,128]{1,0:T(8,128)(2,1)S(1)}, u32[]{:S(2)}, u32[]{:S(2)}) collective-permute-start(bf16[64,128]{1,0:T(8,128)(2,1)S(1)} %fusion.84), channel_id=1, source_target_pairs={{0,8},{4,12},{8,0},{12,4},{16,24},{20,28},{24,16},{28,20},{32,40},... | collective-permute-start | bytes 49160 | tf_op jit(solution)/shard_map/ppermute | solution.py:99
  105.7 2.1 %collective-permute-done.10 = bf16[64,128]{1,0:T(8,128)(2,1)S(1)} collective-permute-done((bf16[64,128]{1,0:T(8,128)(2,1)S(1)}, bf16[64,128]{1,0:T(8,128)(2,1)S(1)}, u32[]{:S(2)}, u32[]{:S(2)}) %collective-permute-start.10) | collective-permute-done | bytes 16416 | tf_op jit(solution)/shard_map/ppermute | solution.py:99
  107.8 9.8 %collective-permute-start.11 = (bf16[128,128]{1,0:T(8,128)(2,1)S(1)}, bf16[128,128]{1,0:T(8,128)(2,1)S(1)}, u32[]{:S(2)}, u32[]{:S(2)}) collective-permute-start(bf16[128,128]{1,0:T(8,128)(2,1)S(1)} %maximum_select_fusion.2), channel_id=1, source_target_pairs={{0,4},{4,0},{8,12},{12,8},{16,20},{20,16},{24,28},{28,24},{32,36},... | collective-permute-start | bytes 98312 | tf_op jit(solution)/shard_map/ppermute | solution.py:99
  117.7 0.8 collective-permute-done.11
  118.5 0.6 maximum_select_fusion.1
  119.1 4.4 %all-to-all-start = ((bf16[64,4,128]{2,1,0:T(4,128)(2,1)}), bf16[64,4,128]{2,1,0:T(4,128)(2,1)S(1)}, u32[]{:S(2)}, u32[]{:S(2)}) async-start(bf16[64,4,128]{2,1,0:T(4,128)(2,1)} %bitcast.20), calls=%async_computation | async-start | bytes 131072 | tf_op jit(solution)/shard_map/all_to_all | solution.py:216
  123.5 15.3 %all_gather.15 = bf16[512,512]{1,0:T(8,128)(2,1)S(1)} all-gather(bf16[128,512]{1,0:T(8,128)(2,1)S(1)} %constant_dynamic-slice_fusion.2), channel_id=1, replica_groups=mesh['seq'=128,'head'=4] {'head'}, dimensions={0}, use_global_device_ids=true | all-gather | bytes 655360 | tf_op jit(solution)/shard_map/all_gather | solution.py:191
  138.8 0.2 fusion.11
  139.0 3.3 %collective-permute-start.12 = (f32[16,4,512]{2,0,1:T(8,128)S(1)}, f32[16,4,512]{2,0,1:T(8,128)S(1)}, u32[]{:S(2)}, u32[]{:S(2)}) collective-permute-start(f32[16,4,512]{2,0,1:T(8,128)S(1)} %fusion.11), channel_id=1, source_target_pairs={{0,4},{4,0},{8,12},{12,8},{16,20},{20,16},{24,28},{28,24},{32,36},... | collective-permute-start | bytes 393224 | tf_op jit(solution)/shard_map/ppermute | solution.py:220
  142.4 1.0 collective-permute-done.12
  143.5 0.2 multiply_reduce_fusion.1
  143.7 0.7 slice_convert_fusion
  144.5 2.2 %fusion.74 = (u8[16,4,256]{2,0,1:T(8,128)(4,1)S(1)}, u8[16,4,256]{2,0,1:T(8,128)(4,1)S(1)}, f32[16,4,4,256]{3,0,2,1:T(8,128)S(1)}) fusion(f32[4,256]{1,0:T(4,128)S(1)} %bitcast.110, bf16[4,1032,256]{2,1,0:T(8,128)(2,1)} %bitcast.112, f32[1024]{0:T(1024)S(1)} %copy-done.10, f32[1024]{0:T(1024)S(1)} %copy-done.11, f32[16,4]{0,1:T(4,128)S(1)} %add_rsqrt_fusion.1, ...), kind=kOutput, calls=%fused_computation.113 | convolution fusion | flops 135823360 | bytes 2802177 | tf_op jit(solution)/shard_map/rtd,hdf->rthf/dot_general | solution.py:230
  146.7 2.5 %convolution_bitcast_fusion = f32[16,4,1024]{2,0,1:T(8,128)S(1)} fusion(bf16[4,256,1024,1]{2,1,0,3:T(8,128)(2,1)} %bitcast.113, f32[16,4,4,256]{3,0,2,1:T(8,128)S(1)} %get-tuple-element.64, u8[16,4,256]{2,0,1:T(8,128)(4,1)S(1)} %get-tuple-element.6, u8[16,4,256]{2,0,1:T(8,128)(4,1)S(1)} %get-tuple-element.5), kind=kOutput, calls=%fused_computation.8 | convolution fusion | flops 138805248 | bytes 2654208 | tf_op jit(solution)/shard_map/rthf,hfd->rtd/dot_general | solution.py:234
  149.3 2.3 %collective-permute-start.13 = (f32[16,4,1024]{2,0,1:T(8,128)S(1)}, f32[16,4,1024]{2,0,1:T(8,128)S(1)}, u32[]{:S(2)}, u32[]{:S(2)}) collective-permute-start(f32[16,4,1024]{2,0,1:T(8,128)S(1)} %convolution_bitcast_fusion), channel_id=1, source_target_pairs={{0,4},{4,0},{8,12},{12,8},{16,20},{20,16},{24,28},{28,24},{32,36},... | collective-permute-start | bytes 786440 | tf_op jit(solution)/shard_map/ppermute | solution.py:235
  151.5 1.2 collective-permute-done.13
  152.7 0.2 fusion.138
  152.9 0.2 multiply_reduce_fusion
  153.3 0.8 copy.264
  (216 shorter events, 11.7 us)
Async XLA Ops:
  6.5 22.4 %copy-start = (bf16[1024,512]{1,0:T(8,128)(2,1)S(1)}, bf16[1024,512]{1,0:T(8,128)(2,1)}, u32[]{:S(2)}) copy-start(bf16[1024,512]{1,0:T(8,128)(2,1)} %param.32) | copy-start | bytes 3145732
  6.5 18.0 %copy-start.18 = (s32[64]{0:T(128)S(1)}, s32[64]{0:T(128)}, u32[]{:S(2)}) copy-start(s32[64]{0:T(128)} %param.24) | copy-start | bytes 772
  6.5 137.1 %all-gather.5.cloned.1.call-start = ((), (), s32[]{:S(2)}) async-start(), calls=%async_computation.1 | async-start | bytes 2641920 | tf_op jit(solution)/shard_map/all_gather | solution.py:203
  6.5 22.4 %collective-permute-start = (bf16[16,4,1024]{2,1,0:T(4,128)(2,1)}, bf16[16,4,1024]{2,1,0:T(4,128)(2,1)S(1)}, u32[]{:S(2)}, u32[]{:S(2)}) collective-permute-start(bf16[16,4,1024]{2,1,0:T(4,128)(2,1)} %param.19), channel_id=1, source_target_pairs={{0,1},{1,2},{2,3},{3,0},{4,5},{5,6},{6,7},{7,4},{8,9},{9,10},{10,1... | collective-permute-start | bytes 393224 | tf_op jit(solution)/shard_map/ppermute | solution.py:113
  10.6 18.4 %collective-permute-start.1 = (bf16[16,4,1024]{2,1,0:T(4,128)(2,1)}, bf16[16,4,1024]{2,1,0:T(4,128)(2,1)S(1)}, u32[]{:S(2)}, u32[]{:S(2)}) collective-permute-start(bf16[16,4,1024]{2,1,0:T(4,128)(2,1)} %param.19), channel_id=1, source_target_pairs={{0,2},{1,3},{2,0},{3,1},{4,6},{5,7},{6,4},{7,5},{8,10},{9,11},{10,... | collective-permute-start | bytes 393224 | tf_op jit(solution)/shard_map/ppermute | solution.py:113
  15.0 14.0 %collective-permute-start.2 = (bf16[16,4,1024]{2,1,0:T(4,128)(2,1)}, bf16[16,4,1024]{2,1,0:T(4,128)(2,1)S(1)}, u32[]{:S(2)}, u32[]{:S(2)}) collective-permute-start(bf16[16,4,1024]{2,1,0:T(4,128)(2,1)} %param.19), channel_id=1, source_target_pairs={{0,3},{1,0},{2,1},{3,2},{4,7},{5,4},{6,5},{7,6},{8,11},{9,8},{10,9... | collective-permute-start | bytes 393224 | tf_op jit(solution)/shard_map/ppermute | solution.py:113
  18.9 7.8 %copy-start.2 = (bf16[64,32,128]{2,1,0:T(8,128)(2,1)S(1)}, bf16[64,32,128]{2,1,0:T(8,128)(2,1)}, u32[]{:S(2)}) copy-start(bf16[64,32,128]{2,1,0:T(8,128)(2,1)} %param.21) | copy-start | bytes 1572868
  24.6 10.7 %copy-start.14 = (pred[4,4]{1,0:T(4,128)(4,1)}, pred[4,4]{1,0:T(4,128)(4,1)S(1)}, u32[]{:S(2)}) copy-start(pred[4,4]{1,0:T(4,128)(4,1)S(1)} %iota_compare_fusion.3) | copy-start | bytes 52
  24.7 5.0 %copy-start.1 = (bf16[16,4,1024]{2,1,0:T(4,128)(2,1)S(1)}, bf16[16,4,1024]{2,1,0:T(4,128)(2,1)}, u32[]{:S(2)}) copy-start(bf16[16,4,1024]{2,1,0:T(4,128)(2,1)} %param.19) | copy-start | bytes 393220
  29.0 0.7 copy-start.4
  41.3 1.3 copy-start.8
  41.3 1.3 copy-start.7
  41.3 8.0 %copy-start.15 = (bf16[1,256]{1,0:T(2,128)(2,1)S(1)}, bf16[1,256]{1,0:T(2,128)(2,1)}, u32[]{:S(2)}) copy-start(bf16[1,256]{1,0:T(2,128)(2,1)} %stack.36) | copy-start | bytes 1540
  41.3 8.0 %copy-start.16 = (bf16[1,256]{1,0:T(2,128)(2,1)S(1)}, bf16[1,256]{1,0:T(2,128)(2,1)}, u32[]{:S(2)}) copy-start(bf16[1,256]{1,0:T(2,128)(2,1)} %stack.37) | copy-start | bytes 1540
  41.3 8.0 %copy-start.17 = (bf16[1,256]{1,0:T(2,128)(2,1)S(1)}, bf16[1,256]{1,0:T(2,128)(2,1)}, u32[]{:S(2)}) copy-start(bf16[1,256]{1,0:T(2,128)(2,1)} %stack.38) | copy-start | bytes 1540
  42.9 7.3 %collective-permute-start.3 = (f32[132,128]{1,0:T(8,128)S(1)}, f32[132,128]{1,0:T(8,128)S(1)}, u32[]{:S(2)}, u32[]{:S(2)}) collective-permute-start(f32[132,128]{1,0:T(8,128)S(1)} %pad_maximum_fusion.2), channel_id=1, source_target_pairs={{0,4},{4,0},{8,12},{12,8},{16,20},{20,16},{24,28},{28,24},{32,36},... | collective-permute-start | bytes 202760 | tf_op jit(solution)/shard_map/ppermute | solution.py:63
  51.1 4.7 %collective-permute-start.4 = (f32[66,128]{1,0:T(8,128)S(1)}, f32[66,128]{1,0:T(8,128)S(1)}, u32[]{:S(2)}, u32[]{:S(2)}) collective-permute-start(f32[66,128]{1,0:T(8,128)S(1)} %pad_maximum_fusion.3), channel_id=1, source_target_pairs={{0,8},{4,12},{8,0},{12,4},{16,24},{20,28},{24,16},{28,20},{32,40},... | collective-permute-start | bytes 101384 | tf_op jit(solution)/shard_map/ppermute | solution.py:63
  53.9 38.4 %copy-start.3 = (bf16[512,1024]{1,0:T(8,128)(2,1)S(1)}, bf16[512,1024]{1,0:T(8,128)(2,1)}, u32[]{:S(2)}) copy-start(bf16[512,1024]{1,0:T(8,128)(2,1)} %param.34) | copy-start | bytes 3145732
  53.9 92.7 %all-gather.7.cloned.1.call-start = ((), (), s32[]{:S(2)}) async-start(), calls=%async_computation.2 | async-start | bytes 2621440 | tf_op jit(solution)/shard_map/all_gather | solution.py:213
  57.2 5.7 %collective-permute-start.5 = (f32[66,128]{1,0:T(8,128)S(1)}, f32[66,128]{1,0:T(8,128)S(1)}, u32[]{:S(2)}, u32[]{:S(2)}) collective-permute-start(f32[66,128]{1,0:T(8,128)S(1)} %pad_maximum_fusion.4), channel_id=1, source_target_pairs={{0,16},{4,20},{8,24},{12,28},{16,0},{20,4},{24,8},{28,12},{32,48},... | collective-permute-start | bytes 101384 | tf_op jit(solution)/shard_map/ppermute | solution.py:63
  64.2 8.6 %collective-permute-start.6 = (f32[66,128]{1,0:T(8,128)S(1)}, f32[66,128]{1,0:T(8,128)S(1)}, u32[]{:S(2)}, u32[]{:S(2)}) collective-permute-start(f32[66,128]{1,0:T(8,128)S(1)} %pad_maximum_fusion.5), channel_id=1, source_target_pairs={{0,32},{4,36},{8,40},{12,44},{16,48},{20,52},{24,56},{28,60},{32,0... | collective-permute-start | bytes 101384 | tf_op jit(solution)/shard_map/ppermute | solution.py:63
  74.1 13.7 %collective-permute-start.7 = (f32[66,128]{1,0:T(8,128)S(1)}, f32[66,128]{1,0:T(8,128)S(1)}, u32[]{:S(2)}, u32[]{:S(2)}) collective-permute-start(f32[66,128]{1,0:T(8,128)S(1)} %pad_maximum_fusion.6), channel_id=1, source_target_pairs={{0,64},{4,68},{8,72},{12,76},{16,80},{20,84},{24,88},{28,92},{32,9... | collective-permute-start | bytes 101384 | tf_op jit(solution)/shard_map/ppermute | solution.py:63
  88.8 28.9 %copy-start.5 = (bf16[128,1024]{1,0:T(8,128)(2,1)S(1)}, bf16[128,1024]{1,0:T(8,128)(2,1)}, u32[]{:S(2)}) copy-start(bf16[128,1024]{1,0:T(8,128)(2,1)} %param.28) | copy-start | bytes 786436
  89.1 4.7 %collective-permute-start.8 = (f32[66,128]{1,0:T(8,128)S(1)}, f32[66,128]{1,0:T(8,128)S(1)}, u32[]{:S(2)}, u32[]{:S(2)}) collective-permute-start(f32[66,128]{1,0:T(8,128)S(1)} %pad_maximum_fusion.7), channel_id=1, source_target_pairs={{0,128},{4,132},{8,136},{12,140},{16,144},{20,148},{24,152},{28,15... | collective-permute-start | bytes 101384 | tf_op jit(solution)/shard_map/ppermute | solution.py:63
  93.9 49.4 %copy-start.6 = (f32[1024]{0:T(1024)S(1)}, f32[1024]{0:T(1024)}, u32[]{:S(2)}) copy-start(f32[1024]{0:T(1024)} %param.29) | copy-start | bytes 12292
  95.1 49.3 %copy-start.10 = (f32[1024]{0:T(1024)S(1)}, f32[1024]{0:T(1024)}, u32[]{:S(2)}) copy-start(f32[1024]{0:T(1024)} %param.31) | copy-start | bytes 12292
  95.1 49.3 %copy-start.11 = (f32[1024]{0:T(1024)S(1)}, f32[1024]{0:T(1024)}, u32[]{:S(2)}) copy-start(f32[1024]{0:T(1024)} %param.30) | copy-start | bytes 12292
  95.2 6.5 %collective-permute-start.9 = (f32[66,128]{1,0:T(8,128)S(1)}, f32[66,128]{1,0:T(8,128)S(1)}, u32[]{:S(2)}, u32[]{:S(2)}) collective-permute-start(f32[66,128]{1,0:T(8,128)S(1)} %pad_maximum_fusion.8), channel_id=1, source_target_pairs={{0,256},{4,260},{8,264},{12,268},{16,272},{20,276},{24,280},{28,28... | collective-permute-start | bytes 101384 | tf_op jit(solution)/shard_map/ppermute | solution.py:63
  103.0 4.8 %collective-permute-start.10 = (bf16[64,128]{1,0:T(8,128)(2,1)S(1)}, bf16[64,128]{1,0:T(8,128)(2,1)S(1)}, u32[]{:S(2)}, u32[]{:S(2)}) collective-permute-start(bf16[64,128]{1,0:T(8,128)(2,1)S(1)} %fusion.84), channel_id=1, source_target_pairs={{0,8},{4,12},{8,0},{12,4},{16,24},{20,28},{24,16},{28,20},{32,40},... | collective-permute-start | bytes 49160 | tf_op jit(solution)/shard_map/ppermute | solution.py:99
  107.8 10.7 %collective-permute-start.11 = (bf16[128,128]{1,0:T(8,128)(2,1)S(1)}, bf16[128,128]{1,0:T(8,128)(2,1)S(1)}, u32[]{:S(2)}, u32[]{:S(2)}) collective-permute-start(bf16[128,128]{1,0:T(8,128)(2,1)S(1)} %maximum_select_fusion.2), channel_id=1, source_target_pairs={{0,4},{4,0},{8,12},{12,8},{16,20},{20,16},{24,28},{28,24},{32,36},... | collective-permute-start | bytes 98312 | tf_op jit(solution)/shard_map/ppermute | solution.py:99
  119.1 19.7 %all-to-all-start = ((bf16[64,4,128]{2,1,0:T(4,128)(2,1)}), bf16[64,4,128]{2,1,0:T(4,128)(2,1)S(1)}, u32[]{:S(2)}, u32[]{:S(2)}) async-start(bf16[64,4,128]{2,1,0:T(4,128)(2,1)} %bitcast.20), calls=%async_computation | async-start | bytes 131072 | tf_op jit(solution)/shard_map/all_to_all | solution.py:216
  139.0 4.3 %collective-permute-start.12 = (f32[16,4,512]{2,0,1:T(8,128)S(1)}, f32[16,4,512]{2,0,1:T(8,128)S(1)}, u32[]{:S(2)}, u32[]{:S(2)}) collective-permute-start(f32[16,4,512]{2,0,1:T(8,128)S(1)} %fusion.11), channel_id=1, source_target_pairs={{0,4},{4,0},{8,12},{12,8},{16,20},{20,16},{24,28},{28,24},{32,36},... | collective-permute-start | bytes 393224 | tf_op jit(solution)/shard_map/ppermute | solution.py:220
  146.7 6.0 %copy-start.9 = (f32[1024]{0:T(1024)S(1)}, f32[1024]{0:T(1024)}, u32[]{:S(2)}) copy-start(f32[1024]{0:T(1024)} %param.35) | copy-start | bytes 12292
  146.7 6.4 %copy-start.12 = (f32[1024]{0:T(1024)S(1)}, f32[1024]{0:T(1024)}, u32[]{:S(2)}) copy-start(f32[1024]{0:T(1024)} %param.37) | copy-start | bytes 12292
  146.7 6.4 %copy-start.13 = (f32[1024]{0:T(1024)S(1)}, f32[1024]{0:T(1024)}, u32[]{:S(2)}) copy-start(f32[1024]{0:T(1024)} %param.36) | copy-start | bytes 12292
  149.3 3.4 %collective-permute-start.13 = (f32[16,4,1024]{2,0,1:T(8,128)S(1)}, f32[16,4,1024]{2,0,1:T(8,128)S(1)}, u32[]{:S(2)}, u32[]{:S(2)}) collective-permute-start(f32[16,4,1024]{2,0,1:T(8,128)S(1)} %convolution_bitcast_fusion), channel_id=1, source_target_pairs={{0,4},{4,0},{8,12},{12,8},{16,20},{20,16},{24,28},{28,24},{32,36},... | collective-permute-start | bytes 786440 | tf_op jit(solution)/shard_map/ppermute | solution.py:235
Sparse Core Ops, SparseCore 0:
  54.1 38.1 all-gather.4
  94.4 44.8 all-gather.6
